TPU v7x, 512 devices: a whole 4x4x16 slice. The times are simulated.
512 devices in a mesh: dp: 4 (over z_hi, core), tm: 8 (over z_lo), height: 16 (over x, y).
Axes of the slice: x: 4, y: 4, z: 16 (z_hi: 2, z_lo: 8; z = z_hi * 8 + z_lo), core: 2. Of those that a mesh axis runs over, the one named last changes fastest.
Arguments:
- clips: bfloat16 [4, 16, 64, 128, 128], P('dp', 'tm', 'height'), may hold values from -6 to 6
- frame_counts: int32 [4, 5], P('dp'), may hold values from 1 to 9, 16 in all within a row
- conv_first: bfloat16 [3, 3, 3, 128, 128], replicated, may hold values from -0.109375 to 0.109375
- conv_down: bfloat16 [3, 3, 3, 128, 128], replicated, may hold values from -0.109375 to 0.109375
- out_cotangent: bfloat16 [4, 8, 32, 64, 128], P('dp', 'tm', 'height'), may hold values from -6 to 6
Outputs:
- encoded: bfloat16 [4, 8, 32, 64, 128], P('dp', 'tm', 'height')
- grad_first: bfloat16 [3, 3, 3, 128, 128], P(None, None, None, 'dp')
- grad_down: bfloat16 [3, 3, 3, 128, 128], P(None, None, None, 'dp')
Inputs may be any that keep to these rules, and one draw needn't show every extreme that they name: `frame_counts`: each sequence's 5 clip lengths sum to 16; in every sequence one clip has exactly 9 frames.
All inputs are finite; a program needn't handle non-finite values.
Results may differ from a plain program's by a relative error of at most 0.0059.
Values may be sent and summed in bfloat16 or wider, within the bound.
No kernel may reach another device: no remote copies, remote signals or barrier semaphores. Data moves between devices by JAX's collectives and lax.ppermute only.
A program may use at most 64 MiB of HBM per device.

v0:
```python
import math

import jax
import jax.numpy as jnp
from jax import lax
from jax.sharding import PartitionSpec as P


def padded_2(cells, sides, width):
    for axis, dim in sides:
        count = lax.axis_size(axis)
        ends = count - 1
        head = lax.slice_in_dim(cells, 0, width, axis=dim)
        tail = lax.slice_in_dim(cells, cells.shape[dim] - width, cells.shape[dim], axis=dim)
        cells = jnp.concatenate(
            [
                lax.ppermute(tail, axis, [(i, (i + 1) % count) for i in range(ends)]),
                cells,
                lax.ppermute(head, axis, [((i + 1) % count, i) for i in range(ends)]),
            ],
            axis=dim,
        )
    return cells


def shifted(value, axis, steps):
    count = lax.axis_size(axis)
    leading, last = (max(0, -steps), min(count, count - steps))
    return lax.ppermute(value, axis, [(source, source + steps) for source in range(leading, last)])


def unfold(frame_slab, stride, pad_cols):
    padded = jnp.pad(frame_slab, ((0, 0), (0, 0), pad_cols, (0, 0)))
    out_rows = (padded.shape[1] - 3) // stride + 1
    out_cols = (padded.shape[2] - 3) // stride + 1
    pieces = []
    for tap_row in range(3):
        for tap_col in range(3):
            pieces.append(
                padded[
                    :,
                    tap_row : tap_row + stride * (out_rows - 1) + 1 : stride,
                    tap_col : tap_col + stride * (out_cols - 1) + 1 : stride,
                ]
            )
    joined = jnp.concatenate(pieces, axis=-1)
    return (joined.reshape(-1, joined.shape[-1]), (frame_slab.shape[0], out_rows, out_cols))


def conv_layer(extended, weight, tap_mask, out_frames, stride, pad_cols):
    channels_out = weight.shape[-1]
    summed = None
    for tap_time in range(3):
        frame_slab = extended[tap_time : tap_time + stride * (out_frames - 1) + 1 : stride]
        columns, shape_out = unfold(frame_slab, stride, pad_cols)
        kernel = weight[tap_time].reshape(-1, channels_out)
        tap_term = jnp.dot(columns, kernel, preferred_element_type=jnp.float32).reshape(
            shape_out + (channels_out,)
        )
        tap_term = tap_term * tap_mask[:, tap_time][:, None, None, None]
        summed = tap_term if summed is None else summed + tap_term
    return summed


def weight_grad(extended, grads, tap_mask, stride, pad_cols):
    out_frames = grads.shape[0]
    blocks = []
    for tap_time in range(3):
        frame_slab = extended[tap_time : tap_time + stride * (out_frames - 1) + 1 : stride]
        columns, shape_out = unfold(frame_slab, stride, pad_cols)
        masked = grads * tap_mask[:, tap_time].astype(jnp.bfloat16)[:, None, None, None]
        blocks.append(
            jnp.dot(
                columns.T, masked.reshape(-1, grads.shape[-1]), preferred_element_type=jnp.float32
            )
        )
    stacked = jnp.stack(blocks)
    return stacked.reshape(3, 3, 3, extended.shape[-1], grads.shape[-1])


def hidden_grad(grads_ext, weight, mask_ext):
    pieces = []
    for tap_time in range(3):
        masked = grads_ext * mask_ext[:, tap_time].astype(jnp.bfloat16)[:, None, None, None]
        kernel = jnp.transpose(weight[tap_time][::-1, ::-1], (0, 1, 3, 2))
        spread = lax.conv_general_dilated(
            masked,
            kernel,
            (1, 1),
            ((2, 0), (2, 2)),
            lhs_dilation=(2, 2),
            dimension_numbers=("NHWC", "HWIO", "NHWC"),
            preferred_element_type=jnp.float32,
        )
        pieces.append(spread[:, 1:, 1:])
    even_frames = pieces[2][:-1] + pieces[0][1:]
    odd_frames = pieces[1][1:]
    merged = jnp.stack([even_frames, odd_frames], axis=1)
    return merged.reshape((2 * even_frames.shape[0],) + even_frames.shape[1:])


def positions(counts_row, frame_index):
    starts = jnp.cumsum(counts_row) - counts_row
    latest = jnp.max(jnp.where(starts[None, :] <= frame_index[:, None], starts[None, :], 0), axis=1)
    return frame_index - latest


def tap_masks(place):
    return (place[:, None] >= (2 - jnp.arange(3, dtype=jnp.int32))[None, :]).astype(jnp.float32)


def body(clips, frame_counts, conv_first, conv_down, out_cotangent):
    frames_dev = clips.shape[1]
    rows_dev = clips.shape[2]
    columns_all = clips.shape[3]
    down_frames = frames_dev // 2
    counts_row = frame_counts[0]
    first_frame = lax.axis_index("tm") * frames_dev
    frame_index = first_frame + jnp.arange(frames_dev, dtype=jnp.int32)
    first_mask = tap_masks(positions(counts_row, frame_index))
    down_index = first_frame + 2 * jnp.arange(down_frames + 1, dtype=jnp.int32)
    mask_ext = tap_masks(positions(counts_row, down_index))
    down_mask = mask_ext[:down_frames]
    with_rows = padded_2(clips[0], (("height", 1),), 1)
    earlier = shifted(with_rows, "tm", 1)
    input_ext = jnp.concatenate([earlier, with_rows], axis=0)
    pre_act = conv_layer(input_ext, conv_first, first_mask, frames_dev, 1, (1, 1))
    hidden = jax.nn.silu(pre_act).astype(jnp.bfloat16)
    above = shifted(hidden[:, rows_dev - 1 :], "height", 1)
    hidden_rows = jnp.concatenate([above, hidden], axis=1)
    hidden_past = shifted(hidden_rows, "tm", 1)
    hidden_ext = jnp.concatenate([hidden_past, hidden_rows], axis=0)
    encoded = conv_layer(hidden_ext, conv_down, down_mask, down_frames, 2, (1, 0)).astype(
        jnp.bfloat16
    )
    cells_all = (
        lax.axis_size("dp")
        * clips.shape[0]
        * down_frames
        * lax.axis_size("tm")
        * (rows_dev // 2)
        * lax.axis_size("height")
        * (columns_all // 2)
    )
    scale = 1.0 / math.sqrt(cells_all)
    grads = (out_cotangent[0].astype(jnp.float32) * scale).astype(jnp.bfloat16)
    down_local = weight_grad(hidden_ext, grads, down_mask, 2, (1, 0))
    below = shifted(grads[:, 0:1], "height", -1)
    grads_rows = jnp.concatenate([grads, below], axis=1)
    grads_next = shifted(grads_rows, "tm", -1)
    grads_ext = jnp.concatenate([grads_rows, grads_next], axis=0)
    back_hidden = hidden_grad(grads_ext, conv_down, mask_ext).astype(jnp.bfloat16)
    sigma = jax.nn.sigmoid(pre_act)
    pre_grad = (back_hidden.astype(jnp.float32) * sigma * (1.0 + pre_act * (1.0 - sigma))).astype(
        jnp.bfloat16
    )
    first_local = weight_grad(input_ext, pre_grad, first_mask, 1, (1, 1))
    share = conv_first.shape[3] // lax.axis_size("dp")
    summed_first, summed_down = lax.psum((first_local, down_local), ("dp", "tm", "height"))
    offset = lax.axis_index("dp") * share
    summed_first = lax.dynamic_slice_in_dim(summed_first, offset, share, 3)
    summed_down = lax.dynamic_slice_in_dim(summed_down, offset, share, 3)
    return (encoded[None], summed_first.astype(jnp.bfloat16), summed_down.astype(jnp.bfloat16))


def solution(mesh):
    in_specs = (
        P("dp", "tm", "height", None, None),
        P("dp", None),
        P(),
        P(),
        P("dp", "tm", "height", None, None),
    )
    out_specs = (
        P("dp", "tm", "height", None, None),
        P(None, None, None, "dp", None),
        P(None, None, None, "dp", None),
    )
    return jax.shard_map(body, mesh=mesh, in_specs=in_specs, out_specs=out_specs, check_vma=False)
```

profile of v0, /device:TPU:6, one launch (start us, length us, event | category | flops | bytes accessed | tf_op | source)
XLA Modules:
  0.0 261.3 jit_solution(3750914941561490961)
XLA Ops:
  0.6 1.0 fusion.93
  1.6 3.5 %collective-permute-start = (bf16[2,1,128,128]{3,2,1,0:T(8,128)(2,1)S(1)}, bf16[2,1,128,128]{3,2,1,0:T(8,128)(2,1)S(1)}, u32[]{:S(2)}, u32[]{:S(2)}) collective-permute-start(bf16[2,1,128,128]{3,2,1,0:T(8,128)(2,1)S(1)} %get-tuple-element.17), channel_id=1, source_target_pairs={{0,1},{1,2},{2,3},{3,4},{4,5},{5,6},{6,7},{7,8},{8,9},{9,10},{10,1... | collective-permute-start | bytes 196616 | tf_op jit(solution)/shard_map/ppermute | solution.py:17
  5.1 4.5 %collective-permute-start.1 = (bf16[2,1,128,128]{3,2,1,0:T(8,128)(2,1)S(1)}, bf16[2,1,128,128]{3,2,1,0:T(8,128)(2,1)S(1)}, u32[]{:S(2)}, u32[]{:S(2)}) collective-permute-start(bf16[2,1,128,128]{3,2,1,0:T(8,128)(2,1)S(1)} %get-tuple-element.18), channel_id=1, source_target_pairs={{1,0},{2,1},{3,2},{4,3},{5,4},{6,5},{7,6},{8,7},{9,8},{10,9},{11,1... | collective-permute-start | bytes 196616 | tf_op jit(solution)/shard_map/ppermute | solution.py:19
  9.6 0.8 fusion.63
  10.4 3.1 %collective-permute-start.5 = (bf16[1,1,64,128]{3,2,1,0:T(8,128)(2,1)S(1)}, bf16[1,1,64,128]{3,2,1,0:T(8,128)(2,1)S(1)}, u32[]{:S(2)}, u32[]{:S(2)}) collective-permute-start(bf16[1,1,64,128]{3,2,1,0:T(8,128)(2,1)S(1)} %slice.442), channel_id=1, source_target_pairs={{1,0},{2,1},{3,2},{4,3},{5,4},{6,5},{7,6},{8,7},{9,8},{10,9},{11,1... | collective-permute-start | bytes 49160 | tf_op jit(solution)/shard_map/ppermute | solution.py:29
  13.5 0.8 reduce-window_clone.1
  14.3 0.7 subtract_bitcast_fusion
  15.0 0.2 fusion.68
  15.3 1.2 fusion.91
  16.6 0.9 fusion.90
  17.5 0.5 fusion.94
  18.0 0.6 slice.447
  18.6 0.6 slice.451
  21.0 1.3 collective-permute-start.6
  22.4 4.6 %collective-permute-start.2 = (bf16[2,6,128,128]{3,2,1,0:T(8,128)(2,1)S(1)}, bf16[2,6,128,128]{3,2,1,0:T(8,128)(2,1)S(1)}, u32[]{:S(2)}, u32[]{:S(2)}) collective-permute-start(bf16[2,6,128,128]{3,2,1,0:T(8,128)(2,1)S(1)} %pad_maximum_fusion.3), channel_id=1, source_target_pairs={{0,16},{16,32},{32,48},{48,64},{64,80},{80,96},{96,112},{1,17},{17... | collective-permute-start | bytes 1179656 | tf_op jit(solution)/shard_map/ppermute | solution.py:29
  27.1 1.3 multiply_bitcast_fusion.1
  28.8 0.3 convolution_select_fusion.2
  29.1 0.3 fusion.4
  29.5 0.1 slice_dynamic-update-slice_fusion.10
  29.6 0.1 slice_dynamic-update-slice_fusion.9
  29.8 0.3 fusion.3
  30.2 0.1 slice_dynamic-update-slice_fusion.8
  30.6 0.1 slice_dynamic-update-slice_fusion.7
  30.8 0.1 slice_dynamic-update-slice_fusion.6
  30.9 3.4 %collective-permute-done.2 = bf16[2,6,128,128]{3,2,1,0:T(8,128)(2,1)S(1)} collective-permute-done((bf16[2,6,128,128]{3,2,1,0:T(8,128)(2,1)S(1)}, bf16[2,6,128,128]{3,2,1,0:T(8,128)(2,1)S(1)}, u32[]{:S(2)}, u32[]{:S(2)}) %collective-permute-start.2) | collective-permute-done | bytes 393248 | tf_op jit(solution)/shard_map/ppermute | solution.py:29
  34.6 0.1 slice_dynamic-update-slice_fusion.16
  34.8 0.1 slice_dynamic-update-slice_fusion.15
  35.0 0.1 slice_dynamic-update-slice_fusion.14
  35.1 0.1 slice_dynamic-update-slice_fusion.13
  35.4 0.8 convolution_multiply_fusion.1
  36.3 0.1 slice_dynamic-update-slice_fusion.22
  36.5 0.1 slice_dynamic-update-slice_fusion.21
  36.8 0.1 slice_dynamic-update-slice_fusion.19
  37.0 0.1 slice_dynamic-update-slice_fusion.18
  37.1 0.8 fusion.1
  37.9 0.9 fusion.10
  38.8 2.8 %collective-permute-start.3 = (bf16[2,1,128,128]{3,2,1,0:T(8,128)(2,1)S(1)}, bf16[2,1,128,128]{3,2,1,0:T(8,128)(2,1)S(1)}, u32[]{:S(2)}, u32[]{:S(2)}) collective-permute-start(bf16[2,1,128,128]{3,2,1,0:T(8,128)(2,1)S(1)} %slice.437), channel_id=1, source_target_pairs={{0,1},{1,2},{2,3},{3,4},{4,5},{5,6},{6,7},{7,8},{8,9},{9,10},{10,1... | collective-permute-start | bytes 196616 | tf_op jit(solution)/shard_map/ppermute | solution.py:29
  41.6 0.9 fusion.26
  42.5 0.9 fusion.24
  43.4 0.9 fusion.22
  44.2 0.2 pad_maximum_fusion
  44.4 2.7 %collective-permute-done.3 = bf16[2,1,128,128]{3,2,1,0:T(8,128)(2,1)S(1)} collective-permute-done((bf16[2,1,128,128]{3,2,1,0:T(8,128)(2,1)S(1)}, bf16[2,1,128,128]{3,2,1,0:T(8,128)(2,1)S(1)}, u32[]{:S(2)}, u32[]{:S(2)}) %collective-permute-start.3) | collective-permute-done | bytes 65568 | tf_op jit(solution)/shard_map/ppermute | solution.py:29
  47.8 0.1 slice.408
  48.0 0.1 slice.409
  48.1 0.2 slice.410
  48.4 4.6 %collective-permute-start.4 = (bf16[2,5,128,128]{3,2,1,0:T(8,128)(2,1)S(1)}, bf16[2,5,128,128]{3,2,1,0:T(8,128)(2,1)S(1)}, u32[]{:S(2)}, u32[]{:S(2)}) collective-permute-start(bf16[2,5,128,128]{3,2,1,0:T(8,128)(2,1)S(1)} %pad_maximum_fusion.2), channel_id=1, source_target_pairs={{0,16},{16,32},{32,48},{48,64},{64,80},{80,96},{96,112},{1,17},{17... | collective-permute-start | bytes 983048 | tf_op jit(solution)/shard_map/ppermute | solution.py:29
  53.3 1.1 convolution_bitcast_fusion
  54.4 3.0 %collective-permute-done.4 = bf16[2,5,128,128]{3,2,1,0:T(8,128)(2,1)S(1)} collective-permute-done((bf16[2,5,128,128]{3,2,1,0:T(8,128)(2,1)S(1)}, bf16[2,5,128,128]{3,2,1,0:T(8,128)(2,1)S(1)}, u32[]{:S(2)}, u32[]{:S(2)}) %collective-permute-start.4) | collective-permute-done | bytes 327712 | tf_op jit(solution)/shard_map/ppermute | solution.py:29
  58.1 0.1 slice.396
  58.3 0.1 slice.397
  58.4 0.2 slice.398
  59.4 0.1 slice.384
  59.5 0.1 slice.385
  59.7 0.2 slice.386
  60.5 0.3 convolution_bitcast_fusion.1
  60.8 0.3 copy-done.4
  61.1 0.3 convolution_bitcast_fusion.2
  61.4 1.2 pad_maximum_fusion.1
  62.5 190.2 %all-reduce.8 = (bf16[3,3,3,128,128]{4,3,2,1,0:T(8,128)(2,1)}, bf16[3,3,3,128,128]{4,3,2,1,0:T(8,128)(2,1)}) all-reduce(f32[3,3,3,128,128]{4,3,2,1,0:T(8,128)S(1)} %pad_maximum_fusion, f32[3,3,3,128,128]{4,3,2,1,0:T(8,128)S(1)} %pad_maximum_fusion.1), channel_id=1, replica_groups=mesh['dp'=4,'tm'=8,'height'=16] {'dp','tm','height'}, use_global_device_ids=true, to_apply=%region_3.4 | all-reduce | flops 884736 | bytes 5308416 | tf_op jit(solution)/shard_map/psum | solution.py:159
  252.8 1.7 dynamic-slice_convert_fusion
  254.5 1.6 dynamic-slice_convert_fusion.1
  256.1 1.8 convolution_multiply_fusion.5
  257.9 1.9 fusion.6
  259.9 1.4 fusion.8
  (122 shorter events, 4.6 us)
Async XLA Ops:
  0.6 21.7 %copy-start = (bf16[1,2,4,128,128]{4,3,2,1,0:T(8,128)(2,1)S(1)}, bf16[1,2,4,128,128]{4,3,2,1,0:T(8,128)(2,1)}, u32[]{:S(2)}) copy-start(bf16[1,2,4,128,128]{4,3,2,1,0:T(8,128)(2,1)} %param.5) | copy-start | bytes 786436
  0.6 15.9 %copy-start.6 = (bf16[3,3,3,128,128]{4,3,2,1,0:T(8,128)(2,1)S(1)}, bf16[3,3,3,128,128]{4,3,2,1,0:T(8,128)(2,1)}, u32[]{:S(2)}) copy-start(bf16[3,3,3,128,128]{4,3,2,1,0:T(8,128)(2,1)} %param.8) | copy-start | bytes 2654212
  1.6 20.7 %collective-permute-start = (bf16[2,1,128,128]{3,2,1,0:T(8,128)(2,1)S(1)}, bf16[2,1,128,128]{3,2,1,0:T(8,128)(2,1)S(1)}, u32[]{:S(2)}, u32[]{:S(2)}) collective-permute-start(bf16[2,1,128,128]{3,2,1,0:T(8,128)(2,1)S(1)} %get-tuple-element.17), channel_id=1, source_target_pairs={{0,1},{1,2},{2,3},{3,4},{4,5},{5,6},{6,7},{7,8},{8,9},{9,10},{10,1... | collective-permute-start | bytes 196616 | tf_op jit(solution)/shard_map/ppermute | solution.py:17
  5.1 17.2 %collective-permute-start.1 = (bf16[2,1,128,128]{3,2,1,0:T(8,128)(2,1)S(1)}, bf16[2,1,128,128]{3,2,1,0:T(8,128)(2,1)S(1)}, u32[]{:S(2)}, u32[]{:S(2)}) collective-permute-start(bf16[2,1,128,128]{3,2,1,0:T(8,128)(2,1)S(1)} %get-tuple-element.18), channel_id=1, source_target_pairs={{1,0},{2,1},{3,2},{4,3},{5,4},{6,5},{7,6},{8,7},{9,8},{10,9},{11,1... | collective-permute-start | bytes 196616 | tf_op jit(solution)/shard_map/ppermute | solution.py:19
  10.4 10.6 %collective-permute-start.5 = (bf16[1,1,64,128]{3,2,1,0:T(8,128)(2,1)S(1)}, bf16[1,1,64,128]{3,2,1,0:T(8,128)(2,1)S(1)}, u32[]{:S(2)}, u32[]{:S(2)}) collective-permute-start(bf16[1,1,64,128]{3,2,1,0:T(8,128)(2,1)S(1)} %slice.442), channel_id=1, source_target_pairs={{1,0},{2,1},{3,2},{4,3},{5,4},{6,5},{7,6},{8,7},{9,8},{10,9},{11,1... | collective-permute-start | bytes 49160 | tf_op jit(solution)/shard_map/ppermute | solution.py:29
  16.5 12.2 %copy-start.8 = (pred[8,18]{0,1:T(8,128)(4,1)S(1)}, pred[8,18]{0,1:T(8,128)(4,1)}, u32[]{:S(2)}) copy-start(pred[8,18]{0,1:T(8,128)(4,1)} %constant.62) | copy-start | bytes 436
  21.0 6.1 %collective-permute-start.6 = (bf16[1,3,64,128]{3,2,1,0:T(8,128)(2,1)S(1)}, bf16[1,3,64,128]{3,2,1,0:T(8,128)(2,1)S(1)}, u32[]{:S(2)}, u32[]{:S(2)}) collective-permute-start(bf16[1,3,64,128]{3,2,1,0:T(8,128)(2,1)S(1)} %pad_maximum_fusion.7), channel_id=1, source_target_pairs={{16,0},{32,16},{48,32},{64,48},{80,64},{96,80},{112,96},{17,1},{33... | collective-permute-start | bytes 147464 | tf_op jit(solution)/shard_map/ppermute | solution.py:29
  22.4 12.0 %collective-permute-start.2 = (bf16[2,6,128,128]{3,2,1,0:T(8,128)(2,1)S(1)}, bf16[2,6,128,128]{3,2,1,0:T(8,128)(2,1)S(1)}, u32[]{:S(2)}, u32[]{:S(2)}) collective-permute-start(bf16[2,6,128,128]{3,2,1,0:T(8,128)(2,1)S(1)} %pad_maximum_fusion.3), channel_id=1, source_target_pairs={{0,16},{16,32},{32,48},{48,64},{64,80},{80,96},{96,112},{1,17},{17... | collective-permute-start | bytes 1179656 | tf_op jit(solution)/shard_map/ppermute | solution.py:29
  38.8 8.3 %collective-permute-start.3 = (bf16[2,1,128,128]{3,2,1,0:T(8,128)(2,1)S(1)}, bf16[2,1,128,128]{3,2,1,0:T(8,128)(2,1)S(1)}, u32[]{:S(2)}, u32[]{:S(2)}) collective-permute-start(bf16[2,1,128,128]{3,2,1,0:T(8,128)(2,1)S(1)} %slice.437), channel_id=1, source_target_pairs={{0,1},{1,2},{2,3},{3,4},{4,5},{5,6},{6,7},{7,8},{8,9},{9,10},{10,1... | collective-permute-start | bytes 196616 | tf_op jit(solution)/shard_map/ppermute | solution.py:29
  44.4 8.9 %copy-start.7 = (bf16[1,1,2,64,128]{4,3,2,1,0:T(8,128)(2,1)S(1)}, bf16[1,1,2,64,128]{4,3,2,1,0:T(8,128)(2,1)}, u32[]{:S(2)}) copy-start(bf16[1,1,2,64,128]{4,3,2,1,0:T(8,128)(2,1)} %param.9) | copy-start | bytes 98308
  48.4 9.0 %collective-permute-start.4 = (bf16[2,5,128,128]{3,2,1,0:T(8,128)(2,1)S(1)}, bf16[2,5,128,128]{3,2,1,0:T(8,128)(2,1)S(1)}, u32[]{:S(2)}, u32[]{:S(2)}) collective-permute-start(bf16[2,5,128,128]{3,2,1,0:T(8,128)(2,1)S(1)} %pad_maximum_fusion.2), channel_id=1, source_target_pairs={{0,16},{16,32},{32,48},{48,64},{64,80},{80,96},{96,112},{1,17},{17... | collective-permute-start | bytes 983048 | tf_op jit(solution)/shard_map/ppermute | solution.py:29
  53.2 7.0 %copy-start.1 = (bf16[1,2,64,1152]{3,2,1,0:T(8,128)(2,1)}, bf16[1,2,64,1152]{3,2,1,0:T(8,128)(2,1)S(1)}, u32[]{:S(2)}) copy-start(bf16[1,2,64,1152]{3,2,1,0:T(8,128)(2,1)S(1)} %constant_dynamic-update-slice_fusion.19) | copy-start | bytes 884740
  60.1 0.7 copy-start.3
  60.4 0.7 copy-start.4
  252.8 7.1 %copy-start.2 = (bf16[1,2,64,1152]{3,2,1,0:T(8,128)(2,1)S(1)}, bf16[1,2,64,1152]{3,2,1,0:T(8,128)(2,1)}, u32[]{:S(2)}) copy-start(bf16[1,2,64,1152]{3,2,1,0:T(8,128)(2,1)} %copy-done.1) | copy-start | bytes 884740
  252.8 7.1 %copy-start.5 = (bf16[1,3,3,128,128]{4,3,2,1,0:T(8,128)(2,1)S(1)}, bf16[1,3,3,128,128]{4,3,2,1,0:T(8,128)(2,1)}, u32[]{:S(2)}) copy-start(bf16[1,3,3,128,128]{4,3,2,1,0:T(8,128)(2,1)} %get-tuple-element.7) | copy-start | bytes 884740
where the time goes:
time: 264 us; the launch traced here: 261 us
  blocking collectives  190 us (72%)
  starting transfers between devices  24.2 us (9%)
  local copies, waits for them, and re-layouts  15.7 us (6%)
  matrix products  12.9 us (5%)
  waiting for transfers between devices  9.16 us (3%)
  other arithmetic  5.57 us (2%)
  between operations  3.57 us (1%)
    psum x1, blocking collectives, body(): lax.psum((first_local, down_local), ('dp', 'tm', 'height'))  190 us
    ppermute x5, starting transfers between devices, shifted(): lax.ppermute(value, axis, [(source, source + steps) for source in range(l...  16.3 us
    ppermute x5, waiting for transfers between devices, shifted(): lax.ppermute(value, axis, [(source, source + steps) for source in range(l...  9.16 us
    dot_general x6, matrix products, conv_layer(): jnp.dot(columns, kernel, preferred_element_type=jnp.float32)  7.65 us
  transfers between devices with their start and end apart: 7, of which 3 were waited for; matrix products, arithmetic and copies ran while one was open for 5% of the time, Pallas kernels for 0%

commit v1 on v0

--- a/solution.py
+++ b/solution.py
@@ -156,11 +156,26 @@
     )
     first_local = weight_grad(input_ext, pre_grad, first_mask, 1, (1, 1))
     share = conv_first.shape[3] // lax.axis_size("dp")
-    summed_first, summed_down = lax.psum((first_local, down_local), ("dp", "tm", "height"))
-    offset = lax.axis_index("dp") * share
-    summed_first = lax.dynamic_slice_in_dim(summed_first, offset, share, 3)
-    summed_down = lax.dynamic_slice_in_dim(summed_down, offset, share, 3)
-    return (encoded[None], summed_first.astype(jnp.bfloat16), summed_down.astype(jnp.bfloat16))
+    quarters = lax.axis_size("dp")
+
+    def by_quarter(term):
+        term = term.reshape(27, quarters, share, term.shape[-1])
+        return jnp.transpose(term, (1, 0, 2, 3)).reshape(quarters, -1)
+
+    stacked = jnp.concatenate([by_quarter(first_local), by_quarter(down_local)], axis=1)
+    rows_n, frames_n = lax.axis_size("height"), lax.axis_size("tm")
+    piece = stacked.reshape(quarters, rows_n, frames_n, -1)
+    piece = lax.psum_scatter(piece, "height", scatter_dimension=1, tiled=True)
+    piece = lax.psum_scatter(piece, "tm", scatter_dimension=2, tiled=True)
+    piece = lax.psum_scatter(piece, "dp", scatter_dimension=0, tiled=True)
+    piece = piece.astype(jnp.bfloat16)
+    piece = lax.all_gather(piece, "tm", axis=2, tiled=True)
+    gathered = lax.all_gather(piece, "height", axis=1, tiled=True).reshape(-1)
+    half = gathered.shape[0] // 2
+    kernel_shape = (3, 3, 3, share, conv_first.shape[-1])
+    summed_first = gathered[:half].reshape(kernel_shape)
+    summed_down = gathered[half:].reshape(kernel_shape)
+    return (encoded[None], summed_first, summed_down)
 
 
 def solution(mesh):

time: 264 us -> 462 us (1.75)
  waiting for transfers between devices: 9.16 us -> 255 us
  blocking collectives: 190 us -> 103 us
  local copies, waits for them, and re-layouts: 15.7 us -> 43.2 us
  between operations: 3.57 us -> 16.9 us
    unnamed x0 -> x4, waiting for transfers between devices: none -> 245 us
    psum x1 -> x0, blocking collectives: 190 us -> none  [body(): lax.psum((first_local, down_local), ('dp', 'tm', 'height'))]
    all_gather x0 -> x2, blocking collectives: none -> 70.4 us  [the longest x1 46.8 us: body(): piece = lax.all_gather(piece, 'tm', axis=2, tiled=True)]
    unnamed x0 -> x1, blocking collectives: none -> 32.2 us
    unnamed x69 -> x66, local copies, waits for them, and re-layouts: 2.91 us -> 17 us
    slice x27, local copies, waits for them, and re-layouts: 3.37 us -> 9.5 us  [unfold(): padded[:, tap_row:tap_row + stride * (out_rows - 1) + 1:stride, tap_col:t...]
    concatenate x0 -> x2, local copies, waits for them, and re-layouts: none -> 4.73 us  [body(): jnp.concatenate([by_quarter(first_local), by_quarter(down_local)], axis=1)]
  transfers between devices with their start and end apart: 7 -> 9, of which waited for: 3 -> 5; matrix products, arithmetic and copies ran while one was open for 5% -> 4% of each run, Pallas kernels for 0% -> 0%
where the time goes in v1:
time: 462 us; the launch traced here: 460 us
  waiting for transfers between devices  255 us (55%)
  blocking collectives  103 us (22%)
  local copies, waits for them, and re-layouts  43.2 us (9%)
  starting transfers between devices  24.5 us (5%)
  between operations  16.9 us (4%)
  matrix products  10 us (2%)
  other arithmetic  8.16 us (2%)
    unnamed x4, waiting for transfers between devices  245 us
    all_gather x1, blocking collectives, body(): piece = lax.all_gather(piece, 'tm', axis=2, tiled=True)  46.8 us
    unnamed x1, blocking collectives  32.2 us
    all_gather x1, blocking collectives, body(): gathered = lax.all_gather(piece, 'height', axis=1, tiled=True).reshape(-1)  23.7 us
    unnamed x66, local copies, waits for them, and re-layouts  17 us
    ppermute x5, starting transfers between devices, shifted(): lax.ppermute(value, axis, [(source, source + steps) for source in range(l...  16.4 us
    slice x27, local copies, waits for them, and re-layouts, unfold(): padded[:, tap_row:tap_row + stride * (out_rows - 1) + 1:stride, tap_col:t...  9.5 us
    ppermute x5, waiting for transfers between devices, shifted(): lax.ppermute(value, axis, [(source, source + steps) for source in range(l...  9.48 us
  transfers between devices with their start and end apart: 9, of which 5 were waited for; matrix products, arithmetic and copies ran while one was open for 4% of the time, Pallas kernels for 0%

profile of v1, /device:TPU:6, one launch (start us, length us, event | category | flops | bytes accessed | tf_op | source)
XLA Modules:
  0.0 460.3 jit_solution(5492218654866860973)
XLA Ops:
  7.2 0.9 fusion.92
  8.1 3.5 collective-permute-start
  11.6 4.5 collective-permute-start.1
  16.1 0.8 fusion.60
  16.9 3.1 collective-permute-start.5
  20.0 0.8 reduce-window_clone.1
  20.8 0.7 subtract_bitcast_fusion
  21.8 1.2 fusion.89
  26.7 1.3 collective-permute-start.6
  28.1 4.7 %collective-permute-start.2 = (bf16[2,6,128,128]{3,2,1,0:T(8,128)(2,1)S(1)}, bf16[2,6,128,128]{3,2,1,0:T(8,128)(2,1)S(1)}, u32[]{:S(2)}, u32[]{:S(2)}) collective-permute-start(bf16[2,6,128,128]{3,2,1,0:T(8,128)(2,1)S(1)} %pad_maximum_fusion.4), channel_id=1, source_target_pairs={{0,16},{16,32},{32,48},{48,64},{64,80},{80,96},{96,112},{1,17},{17... | collective-permute-start | bytes 1179656 | tf_op jit(solution)/shard_map/ppermute | solution.py:29
  32.9 1.3 multiply_bitcast_fusion.1
  36.8 3.4 collective-permute-done.2
  41.2 0.8 convolution_multiply_fusion.1
  42.9 0.8 fusion.1
  43.7 0.9 fusion.10
  44.7 0.9 convolution_bitcast_fusion.5
  45.5 0.9 convolution_bitcast_fusion.4
  46.4 0.9 convolution_bitcast_fusion.3
  47.3 2.8 collective-permute-start.3
  50.2 1.4 copy.96
  51.6 1.9 concatenate.66
  53.5 2.1 collective-permute-done.3
  56.9 4.6 collective-permute-start.4
  61.9 3.9 collective-permute-done.4
  66.0 0.7 slice.399
  66.7 0.7 slice.400
  68.0 0.7 slice.402
  69.3 0.7 slice.404
  70.0 0.7 slice.405
  70.7 0.8 slice.406
  71.6 0.7 slice.386
  72.3 0.7 slice.387
  72.9 0.7 slice.388
  74.4 0.8 constant_dynamic-update-slice_fusion.9
  75.2 0.8 constant_dynamic-update-slice_fusion.17
  76.0 0.8 constant_dynamic-update-slice_fusion.16
  76.7 0.8 constant_dynamic-update-slice_fusion.15
  77.5 0.8 constant_dynamic-update-slice_fusion.14
  78.3 0.8 constant_dynamic-update-slice_fusion.13
  79.1 0.8 constant_dynamic-update-slice_fusion.12
  79.8 0.8 constant_dynamic-update-slice_fusion.11
  80.6 0.8 constant_dynamic-update-slice_fusion.10
  81.6 0.8 constant_dynamic-update-slice_fusion.8
  82.4 0.8 constant_dynamic-update-slice_fusion.7
  83.7 1.4 copy.95
  85.1 2.9 concatenate.67
  88.0 3.6 pad_maximum_fusion
  91.7 1.3 dynamic-slice
  93.1 1.3 dynamic-slice.2
  94.3 1.3 dynamic-slice.4
  95.7 0.8 convolution_multiply_fusion.5
  96.5 128.8 %all-reduce.12.cloned.1.call-done = f32[4,16,8,1728]{3,2,1,0:T(8,128)} async-done(((f32[4,16,8,1728]{3,2,1,0:T(8,128)}), f32[4,16,8,1728]{3,2,1,0:T(8,128)}) %all-reduce.12.cloned.1.call-update) | async-done | bytes 3538960
  225.4 1.6 constant_dynamic-slice_fusion.1
  227.0 0.8 copy.71
  227.8 0.9 fusion.6
  228.7 1.4 fusion.8
  230.1 116.5 %all-reduce.14.cloned.1.call-done = f32[4,1,8,1728]{3,0,1,2:T(4,128)} async-done(((f32[4,1,8,1728]{3,0,1,2:T(4,128)}), f32[4,1,8,1728]{3,0,1,2:T(4,128)}) %all-reduce.14.cloned.1.call-update) | async-done | bytes 221200
  346.6 1.4 constant_dynamic-slice_fusion
  348.1 32.2 %all-reduce.8 = bf16[4,1,1,1728]{3,2,1,0:T(2,128)(2,1)S(1)} all-reduce(f32[4,1,1,1728]{3,2,1,0:T(1,128)S(1)} %copy.72), channel_id=4, replica_groups=mesh['dp'=4,'tm'=8,'height'=16] {'dp'}, use_global_device_ids=true, to_apply=%region_5.6.clone | all-reduce | flops 6912 | bytes 41472
  380.3 0.7 fusion.64
  381.0 46.8 %all_gather.6 = bf16[1,1,8,1728]{3,1,0,2:T(2,128)(2,1)S(1)} all-gather(bf16[1,1,1,1728]{3,1,0,2:T(2,128)(2,1)S(1)} %fusion.64), channel_id=1, replica_groups=mesh['dp'=4,'tm'=8,'height'=16] {'tm'}, dimensions={2}, use_global_device_ids=true | all-gather | bytes 31104 | tf_op jit(solution)/shard_map/all_gather | solution.py:172
  427.7 23.7 %all_gather.7 = bf16[1,16,8,1728]{3,2,0,1:T(8,128)(2,1)S(1)} all-gather(bf16[1,1,8,1728]{3,2,0,1:T(8,128)(2,1)S(1)} %copy.74), channel_id=1, replica_groups=mesh['dp'=4,'tm'=8,'height'=16] {'height'}, dimensions={1}, use_global_device_ids=true | all-gather | bytes 470016 | tf_op jit(solution)/shard_map/all_gather | solution.py:173
  451.5 1.0 reshape.211
  452.5 1.0 reshape.212
  (134 shorter events, 11.5 us)
Async XLA Ops:
  7.2 20.8 %copy-start = (bf16[1,2,4,128,128]{4,3,2,1,0:T(8,128)(2,1)S(1)}, bf16[1,2,4,128,128]{4,3,2,1,0:T(8,128)(2,1)}, u32[]{:S(2)}) copy-start(bf16[1,2,4,128,128]{4,3,2,1,0:T(8,128)(2,1)} %param.5) | copy-start | bytes 786436
  7.2 218.2 %all-reduce.12.cloned.1.call-start = ((), (), s32[]{:S(2)}) async-start(), calls=%async_computation | async-start | bytes 7340032
  8.1 19.8 %collective-permute-start = (bf16[2,1,128,128]{3,2,1,0:T(8,128)(2,1)S(1)}, bf16[2,1,128,128]{3,2,1,0:T(8,128)(2,1)S(1)}, u32[]{:S(2)}, u32[]{:S(2)}) collective-permute-start(bf16[2,1,128,128]{3,2,1,0:T(8,128)(2,1)S(1)} %get-tuple-element.17), channel_id=1, source_target_pairs={{0,1},{1,2},{2,3},{3,4},{4,5},{5,6},{6,7},{7,8},{8,9},{9,10},{10,1... | collective-permute-start | bytes 196616 | tf_op jit(solution)/shard_map/ppermute | solution.py:17
  11.6 16.4 %collective-permute-start.1 = (bf16[2,1,128,128]{3,2,1,0:T(8,128)(2,1)S(1)}, bf16[2,1,128,128]{3,2,1,0:T(8,128)(2,1)S(1)}, u32[]{:S(2)}, u32[]{:S(2)}) collective-permute-start(bf16[2,1,128,128]{3,2,1,0:T(8,128)(2,1)S(1)} %get-tuple-element.18), channel_id=1, source_target_pairs={{1,0},{2,1},{3,2},{4,3},{5,4},{6,5},{7,6},{8,7},{9,8},{10,9},{11,1... | collective-permute-start | bytes 196616 | tf_op jit(solution)/shard_map/ppermute | solution.py:19
  16.9 9.8 %collective-permute-start.5 = (bf16[1,1,64,128]{3,2,1,0:T(8,128)(2,1)S(1)}, bf16[1,1,64,128]{3,2,1,0:T(8,128)(2,1)S(1)}, u32[]{:S(2)}, u32[]{:S(2)}) collective-permute-start(bf16[1,1,64,128]{3,2,1,0:T(8,128)(2,1)S(1)} %slice.452), channel_id=1, source_target_pairs={{1,0},{2,1},{3,2},{4,3},{5,4},{6,5},{7,6},{8,7},{9,8},{10,9},{11,1... | collective-permute-start | bytes 49160 | tf_op jit(solution)/shard_map/ppermute | solution.py:29
  26.7 6.2 %collective-permute-start.6 = (bf16[1,3,64,128]{3,2,1,0:T(8,128)(2,1)S(1)}, bf16[1,3,64,128]{3,2,1,0:T(8,128)(2,1)S(1)}, u32[]{:S(2)}, u32[]{:S(2)}) collective-permute-start(bf16[1,3,64,128]{3,2,1,0:T(8,128)(2,1)S(1)} %pad_maximum_fusion.8), channel_id=1, source_target_pairs={{16,0},{32,16},{48,32},{64,48},{80,64},{96,80},{112,96},{17,1},{33... | collective-permute-start | bytes 147464 | tf_op jit(solution)/shard_map/ppermute | solution.py:29
  28.1 6.9 %copy-start.1 = (bf16[3,3,3,128,128]{4,3,2,1,0:T(8,128)(2,1)S(1)}, bf16[3,3,3,128,128]{4,3,2,1,0:T(8,128)(2,1)}, u32[]{:S(2)}) copy-start(bf16[3,3,3,128,128]{4,3,2,1,0:T(8,128)(2,1)} %param.8) | copy-start | bytes 2654212
  28.1 6.9 %copy-start.4 = (pred[8,18]{0,1:T(8,128)(4,1)S(1)}, pred[8,18]{0,1:T(8,128)(4,1)}, u32[]{:S(2)}) copy-start(pred[8,18]{0,1:T(8,128)(4,1)} %constant.53) | copy-start | bytes 436
  28.1 12.1 %collective-permute-start.2 = (bf16[2,6,128,128]{3,2,1,0:T(8,128)(2,1)S(1)}, bf16[2,6,128,128]{3,2,1,0:T(8,128)(2,1)S(1)}, u32[]{:S(2)}, u32[]{:S(2)}) collective-permute-start(bf16[2,6,128,128]{3,2,1,0:T(8,128)(2,1)S(1)} %pad_maximum_fusion.4), channel_id=1, source_target_pairs={{0,16},{16,32},{32,48},{48,64},{64,80},{80,96},{96,112},{1,17},{17... | collective-permute-start | bytes 1179656 | tf_op jit(solution)/shard_map/ppermute | solution.py:29
  47.3 8.3 %collective-permute-start.3 = (bf16[2,1,128,128]{3,2,1,0:T(8,128)(2,1)S(1)}, bf16[2,1,128,128]{3,2,1,0:T(8,128)(2,1)S(1)}, u32[]{:S(2)}, u32[]{:S(2)}) collective-permute-start(bf16[2,1,128,128]{3,2,1,0:T(8,128)(2,1)S(1)} %slice.447), channel_id=1, source_target_pairs={{0,1},{1,2},{2,3},{3,4},{4,5},{5,6},{6,7},{7,8},{8,9},{9,10},{10,1... | collective-permute-start | bytes 196616 | tf_op jit(solution)/shard_map/ppermute | solution.py:29
  51.6 10.0 %copy-start.3 = (bf16[1,1,2,64,128]{4,3,2,1,0:T(8,128)(2,1)S(1)}, bf16[1,1,2,64,128]{4,3,2,1,0:T(8,128)(2,1)}, u32[]{:S(2)}) copy-start(bf16[1,1,2,64,128]{4,3,2,1,0:T(8,128)(2,1)} %param.9) | copy-start | bytes 98308
  56.9 9.0 %collective-permute-start.4 = (bf16[2,5,128,128]{3,2,1,0:T(8,128)(2,1)S(1)}, bf16[2,5,128,128]{3,2,1,0:T(8,128)(2,1)S(1)}, u32[]{:S(2)}, u32[]{:S(2)}) collective-permute-start(bf16[2,5,128,128]{3,2,1,0:T(8,128)(2,1)S(1)} %pad_maximum_fusion.3), channel_id=1, source_target_pairs={{0,16},{16,32},{32,48},{48,64},{64,80},{80,96},{96,112},{1,17},{17... | collective-permute-start | bytes 983048 | tf_op jit(solution)/shard_map/ppermute | solution.py:29
  91.6 3.9 copy-start.2
  91.7 255.0 %all-reduce.14.cloned.1.call-start = ((), (), s32[]{:S(2)}) async-start(), calls=%async_computation.1 | async-start | bytes 458752
Sparse Core Ops, SparseCore 0:
  91.8 133.5 all-reduce.11
  228.3 118.2 all-reduce.13

commit v2 on v1

--- a/solution.py
+++ b/solution.py
@@ -157,25 +157,63 @@
     first_local = weight_grad(input_ext, pre_grad, first_mask, 1, (1, 1))
     share = conv_first.shape[3] // lax.axis_size("dp")
     quarters = lax.axis_size("dp")
+    rows_n, frames_n = lax.axis_size("height"), lax.axis_size("tm")
 
     def by_quarter(term):
         term = term.reshape(27, quarters, share, term.shape[-1])
         return jnp.transpose(term, (1, 0, 2, 3)).reshape(quarters, -1)
 
     stacked = jnp.concatenate([by_quarter(first_local), by_quarter(down_local)], axis=1)
-    rows_n, frames_n = lax.axis_size("height"), lax.axis_size("tm")
-    piece = stacked.reshape(quarters, rows_n, frames_n, -1)
-    piece = lax.psum_scatter(piece, "height", scatter_dimension=1, tiled=True)
-    piece = lax.psum_scatter(piece, "tm", scatter_dimension=2, tiled=True)
-    piece = lax.psum_scatter(piece, "dp", scatter_dimension=0, tiled=True)
-    piece = piece.astype(jnp.bfloat16)
-    piece = lax.all_gather(piece, "tm", axis=2, tiled=True)
-    gathered = lax.all_gather(piece, "height", axis=1, tiled=True).reshape(-1)
+    owned = reduce_to_owner(stacked.reshape(quarters // 2, 2, rows_n, frames_n, -1))
+    piece = owned.astype(jnp.bfloat16)
+    piece = gather_ring(piece, "tm")
+    gathered = gather_ring(piece, "height").reshape(-1)
     half = gathered.shape[0] // 2
     kernel_shape = (3, 3, 3, share, conv_first.shape[-1])
     summed_first = gathered[:half].reshape(kernel_shape)
     summed_down = gathered[half:].reshape(kernel_shape)
     return (encoded[None], summed_first, summed_down)
+
+
+def pair_swap(value, axis, bit):
+    count = lax.axis_size(axis)
+    return lax.ppermute(value, axis, [(i, i ^ bit) for i in range(count)])
+
+
+def scatter_axis(blocks, axis):
+    count = lax.axis_size(axis)
+    me = lax.axis_index(axis)
+    total = lax.dynamic_index_in_dim(blocks, me, 0, keepdims=False)
+    for step in range(1, count):
+        sent = lax.dynamic_index_in_dim(blocks, (me + step) % count, 0, keepdims=False)
+        total = total + lax.ppermute(sent, axis, [(i, (i + step) % count) for i in range(count)])
+    return total
+
+
+def reduce_to_owner(blocks):
+    core = lax.axis_index("dp") % 2
+    mine = lax.dynamic_index_in_dim(blocks, core, 1, keepdims=False)
+    other = lax.dynamic_index_in_dim(blocks, 1 - core, 1, keepdims=False)
+    blocks = mine + pair_swap(other, "dp", 1)
+    blocks = jnp.moveaxis(blocks, 1, 0)
+    blocks = scatter_axis(blocks, "height")
+    blocks = jnp.moveaxis(blocks, 1, 0)
+    blocks = scatter_axis(blocks, "tm")
+    far = lax.axis_index("dp") // 2
+    mine = lax.dynamic_index_in_dim(blocks, far, 0, keepdims=False)
+    other = lax.dynamic_index_in_dim(blocks, 1 - far, 0, keepdims=False)
+    return mine + pair_swap(other, "dp", 2)
+
+
+def gather_ring(piece, axis):
+    count = lax.axis_size(axis)
+    me = lax.axis_index(axis)
+    received = [piece]
+    for step in range(1, count):
+        received.append(lax.ppermute(piece, axis, [(i, (i + step) % count) for i in range(count)]))
+    stacked = jnp.stack(received)
+    order = (me - jnp.arange(count, dtype=jnp.int32)) % count
+    return stacked[order]
 
 
 def solution(mesh):

time: 462 us -> 305 us (0.66)
  waiting for transfers between devices: 255 us -> 21.6 us
  starting transfers between devices: 24.5 us -> 222 us
  blocking collectives: 103 us -> 0 us
  local copies, waits for them, and re-layouts: 43.2 us -> 27.7 us
  between operations: 16.9 us -> 4.93 us
  other arithmetic: 8.16 us -> 13.1 us
    unnamed x4 -> x0, waiting for transfers between devices: 245 us -> none
    ppermute x0 -> x46, starting transfers between devices: none -> 198 us  [the longest x22 92.8 us: scatter_axis(): lax.ppermute(sent, axis, [(i, (i + step) % count) for i in range(count)])]
    all_gather x2 -> x0, blocking collectives: 70.4 us -> none  [the longest x1 46.8 us: body(): piece = lax.all_gather(piece, 'tm', axis=2, tiled=True)]
    unnamed x1 -> x0, blocking collectives: 32.2 us -> none
    ppermute x0 -> x46, waiting for transfers between devices: none -> 12.1 us  [the longest x22 6.9 us: scatter_axis(): lax.ppermute(sent, axis, [(i, (i + step) % count) for i in range(count)])]
    unnamed x66 -> x99, local copies, waits for them, and re-layouts: 17 us -> 7.98 us
    slice x27, local copies, waits for them, and re-layouts: 9.5 us -> 3.37 us  [unfold(): padded[:, tap_row:tap_row + stride * (out_rows - 1) + 1:stride, tap_col:t...]
    concatenate x2 -> x0, local copies, waits for them, and re-layouts: 4.73 us -> none  [body(): jnp.concatenate([by_quarter(first_local), by_quarter(down_local)], axis=1)]
  transfers between devices with their start and end apart: 9 -> 53, of which waited for: 5 -> 8; matrix products, arithmetic and copies ran while one was open for 4% -> 6% of each run, Pallas kernels for 0% -> 0%
where the time goes in v2:
time: 305 us; the launch traced here: 301 us
  starting transfers between devices  222 us (73%)
  local copies, waits for them, and re-layouts  27.7 us (9%)
  waiting for transfers between devices  21.6 us (7%)
  other arithmetic  13.1 us (4%)
  matrix products  11 us (4%)
  between operations  4.93 us (2%)
    ppermute x22, starting transfers between devices, scatter_axis(): lax.ppermute(sent, axis, [(i, (i + step) % count) for i in range(count)])  92.8 us
    ppermute x22, starting transfers between devices, gather_ring(): lax.ppermute(piece, axis, [(i, (i + step) % count) for i in range(count)])  90.5 us
    ppermute x5, starting transfers between devices, shifted(): lax.ppermute(value, axis, [(source, source + steps) for source in range(l...  16.3 us
    ppermute x2, starting transfers between devices, pair_swap(): return lax.ppermute(value, axis, [(i, i ^ bit) for i in range(count)])  14.8 us
    ppermute x5, waiting for transfers between devices, shifted(): lax.ppermute(value, axis, [(source, source + steps) for source in range(l...  9.5 us
    unnamed x99, local copies, waits for them, and re-layouts  7.98 us
    ppermute x22, waiting for transfers between devices, scatter_axis(): lax.ppermute(sent, axis, [(i, (i + step) % count) for i in range(count)])  6.9 us
    dot_general x6, matrix products, conv_layer(): jnp.dot(columns, kernel, preferred_element_type=jnp.float32)  6.59 us
  transfers between devices with their start and end apart: 53, of which 8 were waited for; matrix products, arithmetic and copies ran while one was open for 6% of the time, Pallas kernels for 0%

profile of v2, /device:TPU:6, one launch (start us, length us, event | category | flops | bytes accessed | tf_op | source)
XLA Modules:
  0.0 300.6 jit_solution(10003797508093969057)
XLA Ops:
  1.6 3.5 %collective-permute-start = (bf16[2,1,128,128]{3,2,1,0:T(8,128)(2,1)S(1)}, bf16[2,1,128,128]{3,2,1,0:T(8,128)(2,1)S(1)}, u32[]{:S(2)}, u32[]{:S(2)}) collective-permute-start(bf16[2,1,128,128]{3,2,1,0:T(8,128)(2,1)S(1)} %get-tuple-element.34), channel_id=1, source_target_pairs={{0,1},{1,2},{2,3},{3,4},{4,5},{5,6},{6,7},{7,8},{8,9},{9,10},{10,1... | collective-permute-start | bytes 196616 | tf_op jit(solution)/shard_map/ppermute | solution.py:17
  5.1 4.5 %collective-permute-start.1 = (bf16[2,1,128,128]{3,2,1,0:T(8,128)(2,1)S(1)}, bf16[2,1,128,128]{3,2,1,0:T(8,128)(2,1)S(1)}, u32[]{:S(2)}, u32[]{:S(2)}) collective-permute-start(bf16[2,1,128,128]{3,2,1,0:T(8,128)(2,1)S(1)} %get-tuple-element.35), channel_id=1, source_target_pairs={{1,0},{2,1},{3,2},{4,3},{5,4},{6,5},{7,6},{8,7},{9,8},{10,9},{11,1... | collective-permute-start | bytes 196616 | tf_op jit(solution)/shard_map/ppermute | solution.py:19
  10.3 3.1 %collective-permute-start.5 = (bf16[1,1,64,128]{3,2,1,0:T(8,128)(2,1)S(1)}, bf16[1,1,64,128]{3,2,1,0:T(8,128)(2,1)S(1)}, u32[]{:S(2)}, u32[]{:S(2)}) collective-permute-start(bf16[1,1,64,128]{3,2,1,0:T(8,128)(2,1)S(1)} %slice.456), channel_id=1, source_target_pairs={{1,0},{2,1},{3,2},{4,3},{5,4},{6,5},{7,6},{8,7},{9,8},{10,9},{11,1... | collective-permute-start | bytes 49160 | tf_op jit(solution)/shard_map/ppermute | solution.py:29
  21.6 4.6 %collective-permute-start.2 = (bf16[2,6,128,128]{3,2,1,0:T(8,128)(2,1)S(1)}, bf16[2,6,128,128]{3,2,1,0:T(8,128)(2,1)S(1)}, u32[]{:S(2)}, u32[]{:S(2)}) collective-permute-start(bf16[2,6,128,128]{3,2,1,0:T(8,128)(2,1)S(1)} %pad_maximum_fusion.4), channel_id=1, source_target_pairs={{0,16},{16,32},{32,48},{48,64},{64,80},{80,96},{96,112},{1,17},{17... | collective-permute-start | bytes 1179656 | tf_op jit(solution)/shard_map/ppermute | solution.py:29
  30.1 3.4 %collective-permute-done.2 = bf16[2,6,128,128]{3,2,1,0:T(8,128)(2,1)S(1)} collective-permute-done((bf16[2,6,128,128]{3,2,1,0:T(8,128)(2,1)S(1)}, bf16[2,6,128,128]{3,2,1,0:T(8,128)(2,1)S(1)}, u32[]{:S(2)}, u32[]{:S(2)}) %collective-permute-start.2) | collective-permute-done | bytes 393248 | tf_op jit(solution)/shard_map/ppermute | solution.py:29
  40.7 2.8 collective-permute-start.3
  43.7 2.4 copy.86
  46.1 2.8 collective-permute-done.3
  50.3 4.6 %collective-permute-start.4 = (bf16[2,5,128,128]{3,2,1,0:T(8,128)(2,1)S(1)}, bf16[2,5,128,128]{3,2,1,0:T(8,128)(2,1)S(1)}, u32[]{:S(2)}, u32[]{:S(2)}) collective-permute-start(bf16[2,5,128,128]{3,2,1,0:T(8,128)(2,1)S(1)} %pad_maximum_fusion.3), channel_id=1, source_target_pairs={{0,16},{16,32},{32,48},{48,64},{64,80},{80,96},{96,112},{1,17},{17... | collective-permute-start | bytes 983048 | tf_op jit(solution)/shard_map/ppermute | solution.py:29
  56.0 3.2 %collective-permute-done.4 = bf16[2,5,128,128]{3,2,1,0:T(8,128)(2,1)S(1)} collective-permute-done((bf16[2,5,128,128]{3,2,1,0:T(8,128)(2,1)S(1)}, bf16[2,5,128,128]{3,2,1,0:T(8,128)(2,1)S(1)}, u32[]{:S(2)}, u32[]{:S(2)}) %collective-permute-start.4) | collective-permute-done | bytes 327712 | tf_op jit(solution)/shard_map/ppermute | solution.py:29
  65.2 5.0 %pad_maximum_fusion = f32[4,221184]{1,0:T(4,128)S(1)} fusion(f32[4,110592]{1,0:T(4,128)S(1)} %bitcast.315, f32[4,110592]{1,0:T(4,128)S(1)} %bitcast.314), kind=kLoop, calls=%fused_computation.2 | loop fusion | flops 884736 | bytes 7077888 | tf_op jit(solution)/shard_map/concatenate | solution.py:166
  70.2 4.2 %reshape.361 = f32[2,2,16,8,1728]{4,3,2,1,0:T(8,128)} reshape(f32[4,221184]{1,0:T(4,128)S(1)} %pad_maximum_fusion) | data formatting | bytes 7077888 | tf_op jit(solution)/shard_map/reshape | solution.py:167
  74.4 1.6 dynamic-slice_bitcast_fusion
  76.0 1.9 collective-permute-start.7
  78.2 3.7 %collective-permute-done.7 = f32[2,16,8,1728]{3,2,1,0:T(8,128)} collective-permute-done((f32[2,16,8,1728]{3,2,1,0:T(8,128)S(1)}, f32[2,16,8,1728]{3,2,1,0:T(8,128)}, u32[]{:S(2)}, u32[]{:S(2)}) %collective-permute-start.7) | collective-permute-done | bytes 1769504 | tf_op jit(solution)/shard_map/ppermute | solution.py:180
  81.8 2.2 bitcast_add_fusion
  85.2 2.0 collective-permute-start.10
  87.3 2.8 collective-permute-start.11
  90.1 5.1 %collective-permute-start.12 = (f32[2,8,1728]{2,1,0:T(8,128)}, f32[2,8,1728]{2,1,0:T(8,128)}, u32[]{:S(2)}, u32[]{:S(2)}) collective-permute-start(f32[2,8,1728]{2,1,0:T(8,128)} %get-tuple-element.18), channel_id=1, source_target_pairs={{0,5},{1,6},{2,7},{3,8},{4,9},{5,10},{6,11},{7,12},{8,13},{9,14},{... | collective-permute-start | bytes 331784 | tf_op jit(solution)/shard_map/ppermute | solution.py:189
  95.2 2.1 collective-permute-start.13
  97.3 5.7 %collective-permute-start.14 = (f32[2,8,1728]{2,1,0:T(8,128)}, f32[2,8,1728]{2,1,0:T(8,128)}, u32[]{:S(2)}, u32[]{:S(2)}) collective-permute-start(f32[2,8,1728]{2,1,0:T(8,128)} %get-tuple-element.16), channel_id=1, source_target_pairs={{0,7},{1,8},{2,9},{3,10},{4,11},{5,12},{6,13},{7,14},{8,15},{9,0},... | collective-permute-start | bytes 331784 | tf_op jit(solution)/shard_map/ppermute | solution.py:189
  103.8 3.3 %collective-permute-start.15 = (f32[2,8,1728]{2,1,0:T(8,128)}, f32[2,8,1728]{2,1,0:T(8,128)S(1)}, u32[]{:S(2)}, u32[]{:S(2)}) collective-permute-start(f32[2,8,1728]{2,1,0:T(8,128)} %get-tuple-element.15), channel_id=1, source_target_pairs={{0,8},{1,9},{2,10},{3,11},{4,12},{5,13},{6,14},{7,15},{8,0},{9,1},... | collective-permute-start | bytes 331784 | tf_op jit(solution)/shard_map/ppermute | solution.py:189
  107.1 3.4 %collective-permute-start.16 = (f32[2,8,1728]{2,1,0:T(8,128)}, f32[2,8,1728]{2,1,0:T(8,128)S(1)}, u32[]{:S(2)}, u32[]{:S(2)}) collective-permute-start(f32[2,8,1728]{2,1,0:T(8,128)} %get-tuple-element.14), channel_id=1, source_target_pairs={{0,9},{1,10},{2,11},{3,12},{4,13},{5,14},{6,15},{7,0},{8,1},{9,2},... | collective-permute-start | bytes 331784 | tf_op jit(solution)/shard_map/ppermute | solution.py:189
  110.5 6.6 %collective-permute-start.17 = (f32[2,8,1728]{2,1,0:T(8,128)}, f32[2,8,1728]{2,1,0:T(8,128)S(1)}, u32[]{:S(2)}, u32[]{:S(2)}) collective-permute-start(f32[2,8,1728]{2,1,0:T(8,128)} %get-tuple-element.13), channel_id=1, source_target_pairs={{0,10},{1,11},{2,12},{3,13},{4,14},{5,15},{6,0},{7,1},{8,2},{9,3},... | collective-permute-start | bytes 331784 | tf_op jit(solution)/shard_map/ppermute | solution.py:189
  117.2 5.0 %collective-permute-start.18 = (f32[2,8,1728]{2,1,0:T(8,128)}, f32[2,8,1728]{2,1,0:T(8,128)S(1)}, u32[]{:S(2)}, u32[]{:S(2)}) collective-permute-start(f32[2,8,1728]{2,1,0:T(8,128)} %get-tuple-element.12), channel_id=1, source_target_pairs={{0,11},{1,12},{2,13},{3,14},{4,15},{5,0},{6,1},{7,2},{8,3},{9,4},{... | collective-permute-start | bytes 331784 | tf_op jit(solution)/shard_map/ppermute | solution.py:189
  122.1 1.9 collective-permute-start.19
  124.1 3.4 %collective-permute-start.20 = (f32[2,8,1728]{2,1,0:T(8,128)}, f32[2,8,1728]{2,1,0:T(8,128)S(1)}, u32[]{:S(2)}, u32[]{:S(2)}) collective-permute-start(f32[2,8,1728]{2,1,0:T(8,128)} %get-tuple-element.10), channel_id=1, source_target_pairs={{0,13},{1,14},{2,15},{3,0},{4,1},{5,2},{6,3},{7,4},{8,5},{9,6},{10... | collective-permute-start | bytes 331784 | tf_op jit(solution)/shard_map/ppermute | solution.py:189
  127.5 2.0 collective-permute-start.21
  129.5 5.8 %collective-permute-start.22 = (f32[2,8,1728]{2,1,0:T(8,128)}, f32[2,8,1728]{2,1,0:T(8,128)S(1)}, u32[]{:S(2)}, u32[]{:S(2)}) collective-permute-start(f32[2,8,1728]{2,1,0:T(8,128)} %get-tuple-element.8), channel_id=1, source_target_pairs={{0,15},{1,0},{2,1},{3,2},{4,3},{5,4},{6,5},{7,6},{8,7},{9,8},{10,9... | collective-permute-start | bytes 331784 | tf_op jit(solution)/shard_map/ppermute | solution.py:189
  135.3 1.9 collective-permute-start.8
  137.3 3.5 %collective-permute-start.9 = (f32[2,8,1728]{2,1,0:T(8,128)S(1)}, f32[2,8,1728]{2,1,0:T(8,128)S(1)}, u32[]{:S(2)}, u32[]{:S(2)}) collective-permute-start(f32[2,8,1728]{2,1,0:T(8,128)S(1)} %get-tuple-element.21), channel_id=1, source_target_pairs={{0,2},{1,3},{2,4},{3,5},{4,6},{5,7},{6,8},{7,9},{8,10},{9,11},{10,... | collective-permute-start | bytes 331784 | tf_op jit(solution)/shard_map/ppermute | solution.py:189
  140.8 3.3 %collective-permute-done.8 = f32[2,8,1728]{2,1,0:T(8,128)S(1)} collective-permute-done((f32[2,8,1728]{2,1,0:T(8,128)S(1)}, f32[2,8,1728]{2,1,0:T(8,128)S(1)}, u32[]{:S(2)}, u32[]{:S(2)}) %collective-permute-start.8) | collective-permute-done | bytes 110624 | tf_op jit(solution)/shard_map/ppermute | solution.py:189
  144.1 2.2 collective-permute-done.9
  147.7 4.4 %collective-permute-start.23 = (f32[2,1728]{1,0:T(2,128)S(1)}, f32[2,1728]{1,0:T(2,128)S(1)}, u32[]{:S(2)}, u32[]{:S(2)}) collective-permute-start(f32[2,1728]{1,0:T(2,128)S(1)} %bitcast.339), channel_id=1, source_target_pairs={{0,16},{16,32},{32,48},{48,64},{64,80},{80,96},{96,112},{112,0},{1... | collective-permute-start | bytes 41480 | tf_op jit(solution)/shard_map/ppermute | solution.py:189
  152.1 7.0 %collective-permute-start.24 = (f32[2,1728]{1,0:T(2,128)S(1)}, f32[2,1728]{1,0:T(2,128)S(1)}, u32[]{:S(2)}, u32[]{:S(2)}) collective-permute-start(f32[2,1728]{1,0:T(2,128)S(1)} %bitcast.338), channel_id=1, source_target_pairs={{0,32},{16,48},{32,64},{48,80},{64,96},{80,112},{96,0},{112,16},{1... | collective-permute-start | bytes 41480 | tf_op jit(solution)/shard_map/ppermute | solution.py:189
  159.2 5.9 %collective-permute-start.25 = (f32[2,1728]{1,0:T(2,128)S(1)}, f32[2,1728]{1,0:T(2,128)S(1)}, u32[]{:S(2)}, u32[]{:S(2)}) collective-permute-start(f32[2,1728]{1,0:T(2,128)S(1)} %bitcast.333), channel_id=1, source_target_pairs={{0,48},{16,64},{32,80},{48,96},{64,112},{80,0},{96,16},{112,32},{1... | collective-permute-start | bytes 41480 | tf_op jit(solution)/shard_map/ppermute | solution.py:189
  165.1 3.1 %collective-permute-start.26 = (f32[2,1728]{1,0:T(2,128)S(1)}, f32[2,1728]{1,0:T(2,128)S(1)}, u32[]{:S(2)}, u32[]{:S(2)}) collective-permute-start(f32[2,1728]{1,0:T(2,128)S(1)} %bitcast.334), channel_id=1, source_target_pairs={{0,64},{16,80},{32,96},{48,112},{64,0},{80,16},{96,32},{112,48},{1... | collective-permute-start | bytes 41480 | tf_op jit(solution)/shard_map/ppermute | solution.py:189
  168.2 7.8 %collective-permute-start.27 = (f32[2,1728]{1,0:T(2,128)S(1)}, f32[2,1728]{1,0:T(2,128)S(1)}, u32[]{:S(2)}, u32[]{:S(2)}) collective-permute-start(f32[2,1728]{1,0:T(2,128)S(1)} %bitcast.335), channel_id=1, source_target_pairs={{0,80},{16,96},{32,112},{48,0},{64,16},{80,32},{96,48},{112,64},{1... | collective-permute-start | bytes 41480 | tf_op jit(solution)/shard_map/ppermute | solution.py:189
  176.1 5.3 %collective-permute-start.28 = (f32[2,1728]{1,0:T(2,128)S(1)}, f32[2,1728]{1,0:T(2,128)S(1)}, u32[]{:S(2)}, u32[]{:S(2)}) collective-permute-start(f32[2,1728]{1,0:T(2,128)S(1)} %bitcast.337), channel_id=1, source_target_pairs={{0,96},{16,112},{32,0},{48,16},{64,32},{80,48},{96,64},{112,80},{1... | collective-permute-start | bytes 41480 | tf_op jit(solution)/shard_map/ppermute | solution.py:189
  181.4 4.8 %collective-permute-start.29 = (f32[2,1728]{1,0:T(2,128)S(1)}, f32[2,1728]{1,0:T(2,128)S(1)}, u32[]{:S(2)}, u32[]{:S(2)}) collective-permute-start(f32[2,1728]{1,0:T(2,128)S(1)} %bitcast.336), channel_id=1, source_target_pairs={{0,112},{16,0},{32,16},{48,32},{64,48},{80,64},{96,80},{112,96},{1... | collective-permute-start | bytes 41480 | tf_op jit(solution)/shard_map/ppermute | solution.py:189
  187.7 12.8 %collective-permute-start.30 = (f32[1728]{0:T(1024)S(1)}, f32[1728]{0:T(1024)S(1)}, u32[]{:S(2)}, u32[]{:S(2)}) collective-permute-start(f32[1728]{0:T(1024)S(1)} %get-tuple-element.3), channel_id=1, source_target_pairs={{0,256},{128,384},{256,0},{384,128},{1,257},{129,385},{257,1},{385... | collective-permute-start | bytes 20744 | tf_op jit(solution)/shard_map/ppermute | solution.py:180
  200.6 1.7 convolution_multiply_fusion.5
  202.3 1.9 collective-permute-start.31
  204.3 2.1 collective-permute-start.32
  207.3 6.2 %collective-permute-start.33 = (bf16[1728]{0:T(1024)(128)(2,1)S(1)}, bf16[1728]{0:T(1024)(128)(2,1)S(1)}, u32[]{:S(2)}, u32[]{:S(2)}) collective-permute-start(bf16[1728]{0:T(1024)(128)(2,1)S(1)} %add_convert_fusion), channel_id=1, source_target_pairs={{0,48},{16,64},{32,80},{48,96},{64,112},{80,0},{96,16},{112,32},{1... | collective-permute-start | bytes 10376 | tf_op jit(solution)/shard_map/ppermute | solution.py:213
  213.4 7.7 %collective-permute-start.34 = (bf16[1728]{0:T(1024)(128)(2,1)S(1)}, bf16[1728]{0:T(1024)(128)(2,1)S(1)}, u32[]{:S(2)}, u32[]{:S(2)}) collective-permute-start(bf16[1728]{0:T(1024)(128)(2,1)S(1)} %add_convert_fusion), channel_id=1, source_target_pairs={{0,64},{16,80},{32,96},{48,112},{64,0},{80,16},{96,32},{112,48},{1... | collective-permute-start | bytes 10376 | tf_op jit(solution)/shard_map/ppermute | solution.py:213
  221.1 7.8 %collective-permute-start.35 = (bf16[1728]{0:T(1024)(128)(2,1)S(1)}, bf16[1728]{0:T(1024)(128)(2,1)S(1)}, u32[]{:S(2)}, u32[]{:S(2)}) collective-permute-start(bf16[1728]{0:T(1024)(128)(2,1)S(1)} %add_convert_fusion), channel_id=1, source_target_pairs={{0,80},{16,96},{32,112},{48,0},{64,16},{80,32},{96,48},{112,64},{1... | collective-permute-start | bytes 10376 | tf_op jit(solution)/shard_map/ppermute | solution.py:213
  229.0 1.9 collective-permute-start.36
  230.9 4.3 %collective-permute-start.37 = (bf16[1728]{0:T(1024)(128)(2,1)S(1)}, bf16[1728]{0:T(1024)(128)(2,1)S(1)}, u32[]{:S(2)}, u32[]{:S(2)}) collective-permute-start(bf16[1728]{0:T(1024)(128)(2,1)S(1)} %add_convert_fusion), channel_id=1, source_target_pairs={{0,112},{16,0},{32,16},{48,32},{64,48},{80,64},{96,80},{112,96},{1... | collective-permute-start | bytes 10376 | tf_op jit(solution)/shard_map/ppermute | solution.py:213
  237.5 2.5 collective-permute-start.38
  240.0 5.4 %collective-permute-start.39 = (bf16[8,1728]{1,0:T(8,128)(2,1)S(1)}, bf16[8,1728]{1,0:T(8,128)(2,1)S(1)}, u32[]{:S(2)}, u32[]{:S(2)}) collective-permute-start(bf16[8,1728]{1,0:T(8,128)(2,1)S(1)} %gather_fusion), channel_id=1, source_target_pairs={{0,2},{1,3},{2,4},{3,5},{4,6},{5,7},{6,8},{7,9},{8,10},{9,11},{10,... | collective-permute-start | bytes 82952 | tf_op jit(solution)/shard_map/ppermute | solution.py:213
  245.5 4.3 %collective-permute-start.40 = (bf16[8,1728]{1,0:T(8,128)(2,1)S(1)}, bf16[8,1728]{1,0:T(8,128)(2,1)S(1)}, u32[]{:S(2)}, u32[]{:S(2)}) collective-permute-start(bf16[8,1728]{1,0:T(8,128)(2,1)S(1)} %gather_fusion), channel_id=1, source_target_pairs={{0,3},{1,4},{2,5},{3,6},{4,7},{5,8},{6,9},{7,10},{8,11},{9,12},{10... | collective-permute-start | bytes 82952 | tf_op jit(solution)/shard_map/ppermute | solution.py:213
  249.7 2.7 collective-permute-start.41
  252.5 3.5 %collective-permute-start.42 = (bf16[8,1728]{1,0:T(8,128)(2,1)S(1)}, bf16[8,1728]{1,0:T(8,128)(2,1)S(1)}, u32[]{:S(2)}, u32[]{:S(2)}) collective-permute-start(bf16[8,1728]{1,0:T(8,128)(2,1)S(1)} %gather_fusion), channel_id=1, source_target_pairs={{0,5},{1,6},{2,7},{3,8},{4,9},{5,10},{6,11},{7,12},{8,13},{9,14},{... | collective-permute-start | bytes 82952 | tf_op jit(solution)/shard_map/ppermute | solution.py:213
  255.9 5.4 %collective-permute-start.43 = (bf16[8,1728]{1,0:T(8,128)(2,1)S(1)}, bf16[8,1728]{1,0:T(8,128)(2,1)S(1)}, u32[]{:S(2)}, u32[]{:S(2)}) collective-permute-start(bf16[8,1728]{1,0:T(8,128)(2,1)S(1)} %gather_fusion), channel_id=1, source_target_pairs={{0,6},{1,7},{2,8},{3,9},{4,10},{5,11},{6,12},{7,13},{8,14},{9,15},... | collective-permute-start | bytes 82952 | tf_op jit(solution)/shard_map/ppermute | solution.py:213
  261.4 3.8 %collective-permute-start.44 = (bf16[8,1728]{1,0:T(8,128)(2,1)S(1)}, bf16[8,1728]{1,0:T(8,128)(2,1)S(1)}, u32[]{:S(2)}, u32[]{:S(2)}) collective-permute-start(bf16[8,1728]{1,0:T(8,128)(2,1)S(1)} %gather_fusion), channel_id=1, source_target_pairs={{0,7},{1,8},{2,9},{3,10},{4,11},{5,12},{6,13},{7,14},{8,15},{9,0},... | collective-permute-start | bytes 82952 | tf_op jit(solution)/shard_map/ppermute | solution.py:213
  265.2 3.6 %collective-permute-start.45 = (bf16[8,1728]{1,0:T(8,128)(2,1)S(1)}, bf16[8,1728]{1,0:T(8,128)(2,1)S(1)}, u32[]{:S(2)}, u32[]{:S(2)}) collective-permute-start(bf16[8,1728]{1,0:T(8,128)(2,1)S(1)} %gather_fusion), channel_id=1, source_target_pairs={{0,8},{1,9},{2,10},{3,11},{4,12},{5,13},{6,14},{7,15},{8,0},{9,1},... | collective-permute-start | bytes 82952 | tf_op jit(solution)/shard_map/ppermute | solution.py:213
  268.8 3.4 %collective-permute-start.46 = (bf16[8,1728]{1,0:T(8,128)(2,1)S(1)}, bf16[8,1728]{1,0:T(8,128)(2,1)S(1)}, u32[]{:S(2)}, u32[]{:S(2)}) collective-permute-start(bf16[8,1728]{1,0:T(8,128)(2,1)S(1)} %gather_fusion), channel_id=1, source_target_pairs={{0,9},{1,10},{2,11},{3,12},{4,13},{5,14},{6,15},{7,0},{8,1},{9,2},... | collective-permute-start | bytes 82952 | tf_op jit(solution)/shard_map/ppermute | solution.py:213
  272.2 5.4 %collective-permute-start.47 = (bf16[8,1728]{1,0:T(8,128)(2,1)S(1)}, bf16[8,1728]{1,0:T(8,128)(2,1)S(1)}, u32[]{:S(2)}, u32[]{:S(2)}) collective-permute-start(bf16[8,1728]{1,0:T(8,128)(2,1)S(1)} %gather_fusion), channel_id=1, source_target_pairs={{0,10},{1,11},{2,12},{3,13},{4,14},{5,15},{6,0},{7,1},{8,2},{9,3},... | collective-permute-start | bytes 82952 | tf_op jit(solution)/shard_map/ppermute | solution.py:213
  277.7 3.5 %collective-permute-start.48 = (bf16[8,1728]{1,0:T(8,128)(2,1)S(1)}, bf16[8,1728]{1,0:T(8,128)(2,1)S(1)}, u32[]{:S(2)}, u32[]{:S(2)}) collective-permute-start(bf16[8,1728]{1,0:T(8,128)(2,1)S(1)} %gather_fusion), channel_id=1, source_target_pairs={{0,11},{1,12},{2,13},{3,14},{4,15},{5,0},{6,1},{7,2},{8,3},{9,4},{... | collective-permute-start | bytes 82952 | tf_op jit(solution)/shard_map/ppermute | solution.py:213
  281.2 3.7 %collective-permute-start.49 = (bf16[8,1728]{1,0:T(8,128)(2,1)S(1)}, bf16[8,1728]{1,0:T(8,128)(2,1)S(1)}, u32[]{:S(2)}, u32[]{:S(2)}) collective-permute-start(bf16[8,1728]{1,0:T(8,128)(2,1)S(1)} %gather_fusion), channel_id=1, source_target_pairs={{0,12},{1,13},{2,14},{3,15},{4,0},{5,1},{6,2},{7,3},{8,4},{9,5},{1... | collective-permute-start | bytes 82952 | tf_op jit(solution)/shard_map/ppermute | solution.py:213
  284.9 1.9 collective-permute-start.50
  286.9 4.0 %collective-permute-start.51 = (bf16[8,1728]{1,0:T(8,128)(2,1)S(1)}, bf16[8,1728]{1,0:T(8,128)(2,1)S(1)}, u32[]{:S(2)}, u32[]{:S(2)}) collective-permute-start(bf16[8,1728]{1,0:T(8,128)(2,1)S(1)} %gather_fusion), channel_id=1, source_target_pairs={{0,14},{1,15},{2,0},{3,1},{4,2},{5,3},{6,4},{7,5},{8,6},{9,7},{10,... | collective-permute-start | bytes 82952 | tf_op jit(solution)/shard_map/ppermute | solution.py:213
  290.9 5.5 %collective-permute-start.52 = (bf16[8,1728]{1,0:T(8,128)(2,1)S(1)}, bf16[8,1728]{1,0:T(8,128)(2,1)S(1)}, u32[]{:S(2)}, u32[]{:S(2)}) collective-permute-start(bf16[8,1728]{1,0:T(8,128)(2,1)S(1)} %gather_fusion), channel_id=1, source_target_pairs={{0,15},{1,0},{2,1},{3,2},{4,3},{5,4},{6,5},{7,6},{8,7},{9,8},{10,9... | collective-permute-start | bytes 82952 | tf_op jit(solution)/shard_map/ppermute | solution.py:213
  (269 shorter events, 38.8 us)
Async XLA Ops:
  0.6 20.9 %copy-start = (bf16[1,2,4,128,128]{4,3,2,1,0:T(8,128)(2,1)S(1)}, bf16[1,2,4,128,128]{4,3,2,1,0:T(8,128)(2,1)}, u32[]{:S(2)}) copy-start(bf16[1,2,4,128,128]{4,3,2,1,0:T(8,128)(2,1)} %param.5) | copy-start | bytes 786436
  1.6 19.9 %collective-permute-start = (bf16[2,1,128,128]{3,2,1,0:T(8,128)(2,1)S(1)}, bf16[2,1,128,128]{3,2,1,0:T(8,128)(2,1)S(1)}, u32[]{:S(2)}, u32[]{:S(2)}) collective-permute-start(bf16[2,1,128,128]{3,2,1,0:T(8,128)(2,1)S(1)} %get-tuple-element.34), channel_id=1, source_target_pairs={{0,1},{1,2},{2,3},{3,4},{4,5},{5,6},{6,7},{7,8},{8,9},{9,10},{10,1... | collective-permute-start | bytes 196616 | tf_op jit(solution)/shard_map/ppermute | solution.py:17
  5.1 16.5 %collective-permute-start.1 = (bf16[2,1,128,128]{3,2,1,0:T(8,128)(2,1)S(1)}, bf16[2,1,128,128]{3,2,1,0:T(8,128)(2,1)S(1)}, u32[]{:S(2)}, u32[]{:S(2)}) collective-permute-start(bf16[2,1,128,128]{3,2,1,0:T(8,128)(2,1)S(1)} %get-tuple-element.35), channel_id=1, source_target_pairs={{1,0},{2,1},{3,2},{4,3},{5,4},{6,5},{7,6},{8,7},{9,8},{10,9},{11,1... | collective-permute-start | bytes 196616 | tf_op jit(solution)/shard_map/ppermute | solution.py:19
  10.3 9.9 %collective-permute-start.5 = (bf16[1,1,64,128]{3,2,1,0:T(8,128)(2,1)S(1)}, bf16[1,1,64,128]{3,2,1,0:T(8,128)(2,1)S(1)}, u32[]{:S(2)}, u32[]{:S(2)}) collective-permute-start(bf16[1,1,64,128]{3,2,1,0:T(8,128)(2,1)S(1)} %slice.456), channel_id=1, source_target_pairs={{1,0},{2,1},{3,2},{4,3},{5,4},{6,5},{7,6},{8,7},{9,8},{10,9},{11,1... | collective-permute-start | bytes 49160 | tf_op jit(solution)/shard_map/ppermute | solution.py:29
  15.3 12.7 %copy-start.8 = (bf16[3,3,3,128,128]{4,3,2,1,0:T(8,128)(2,1)S(1)}, bf16[3,3,3,128,128]{4,3,2,1,0:T(8,128)(2,1)}, u32[]{:S(2)}) copy-start(bf16[3,3,3,128,128]{4,3,2,1,0:T(8,128)(2,1)} %param.8) | copy-start | bytes 2654212
  15.3 12.7 %copy-start.11 = (pred[8,18]{0,1:T(8,128)(4,1)S(1)}, pred[8,18]{0,1:T(8,128)(4,1)}, u32[]{:S(2)}) copy-start(pred[8,18]{0,1:T(8,128)(4,1)} %constant.291) | copy-start | bytes 436
  20.2 6.1 %collective-permute-start.6 = (bf16[1,3,64,128]{3,2,1,0:T(8,128)(2,1)S(1)}, bf16[1,3,64,128]{3,2,1,0:T(8,128)(2,1)S(1)}, u32[]{:S(2)}, u32[]{:S(2)}) collective-permute-start(bf16[1,3,64,128]{3,2,1,0:T(8,128)(2,1)S(1)} %pad_maximum_fusion.8), channel_id=1, source_target_pairs={{16,0},{32,16},{48,32},{64,48},{80,64},{96,80},{112,96},{17,1},{33... | collective-permute-start | bytes 147464 | tf_op jit(solution)/shard_map/ppermute | solution.py:29
  21.6 12.0 %collective-permute-start.2 = (bf16[2,6,128,128]{3,2,1,0:T(8,128)(2,1)S(1)}, bf16[2,6,128,128]{3,2,1,0:T(8,128)(2,1)S(1)}, u32[]{:S(2)}, u32[]{:S(2)}) collective-permute-start(bf16[2,6,128,128]{3,2,1,0:T(8,128)(2,1)S(1)} %pad_maximum_fusion.4), channel_id=1, source_target_pairs={{0,16},{16,32},{32,48},{48,64},{64,80},{80,96},{96,112},{1,17},{17... | collective-permute-start | bytes 1179656 | tf_op jit(solution)/shard_map/ppermute | solution.py:29
  40.7 8.3 %collective-permute-start.3 = (bf16[2,1,128,128]{3,2,1,0:T(8,128)(2,1)S(1)}, bf16[2,1,128,128]{3,2,1,0:T(8,128)(2,1)S(1)}, u32[]{:S(2)}, u32[]{:S(2)}) collective-permute-start(bf16[2,1,128,128]{3,2,1,0:T(8,128)(2,1)S(1)} %slice.451), channel_id=1, source_target_pairs={{0,1},{1,2},{2,3},{3,4},{4,5},{5,6},{6,7},{7,8},{8,9},{9,10},{10,1... | collective-permute-start | bytes 196616 | tf_op jit(solution)/shard_map/ppermute | solution.py:29
  43.7 12.0 %copy-start.10 = (bf16[1,1,2,64,128]{4,3,2,1,0:T(8,128)(2,1)S(1)}, bf16[1,1,2,64,128]{4,3,2,1,0:T(8,128)(2,1)}, u32[]{:S(2)}) copy-start(bf16[1,1,2,64,128]{4,3,2,1,0:T(8,128)(2,1)} %param.9) | copy-start | bytes 98308
  50.3 9.0 %collective-permute-start.4 = (bf16[2,5,128,128]{3,2,1,0:T(8,128)(2,1)S(1)}, bf16[2,5,128,128]{3,2,1,0:T(8,128)(2,1)S(1)}, u32[]{:S(2)}, u32[]{:S(2)}) collective-permute-start(bf16[2,5,128,128]{3,2,1,0:T(8,128)(2,1)S(1)} %pad_maximum_fusion.3), channel_id=1, source_target_pairs={{0,16},{16,32},{32,48},{48,64},{64,80},{80,96},{96,112},{1,17},{17... | collective-permute-start | bytes 983048 | tf_op jit(solution)/shard_map/ppermute | solution.py:29
  55.0 0.7 copy-start.4
  62.4 0.7 copy-start.2
  63.7 1.5 copy-start.1
  76.0 5.8 %collective-permute-start.7 = (f32[2,16,8,1728]{3,2,1,0:T(8,128)S(1)}, f32[2,16,8,1728]{3,2,1,0:T(8,128)}, u32[]{:S(2)}, u32[]{:S(2)}) collective-permute-start(f32[2,16,8,1728]{3,2,1,0:T(8,128)S(1)} %dynamic-slice_bitcast_fusion), channel_id=1, source_target_pairs={{0,128},{128,0},{256,384},{384,256},{1,129},{129,1},{257,385},{385... | collective-permute-start | bytes 5308424 | tf_op jit(solution)/shard_map/ppermute | solution.py:180
  84.1 18.9 %copy-start.9 = (bf16[3,3,3,128,128]{4,3,2,1,0:T(8,128)(2,1)S(1)}, bf16[3,3,3,128,128]{4,3,2,1,0:T(8,128)(2,1)}, u32[]{:S(2)}) copy-start(bf16[3,3,3,128,128]{4,3,2,1,0:T(8,128)(2,1)} %param.8) | copy-start | bytes 2654212
  85.2 115.3 %copy-start.3 = (bf16[1,2,64,1152]{3,2,1,0:T(8,128)(2,1)S(1)}, bf16[1,2,64,1152]{3,2,1,0:T(8,128)(2,1)}, u32[]{:S(2)}) copy-start(bf16[1,2,64,1152]{3,2,1,0:T(8,128)(2,1)} %copy-done.2) | copy-start | bytes 884740
  85.2 18.5 %collective-permute-start.10 = (f32[2,8,1728]{2,1,0:T(8,128)}, f32[2,8,1728]{2,1,0:T(8,128)}, u32[]{:S(2)}, u32[]{:S(2)}) collective-permute-start(f32[2,8,1728]{2,1,0:T(8,128)} %get-tuple-element.20), channel_id=1, source_target_pairs={{0,3},{1,4},{2,5},{3,6},{4,7},{5,8},{6,9},{7,10},{8,11},{9,12},{10... | collective-permute-start | bytes 331784 | tf_op jit(solution)/shard_map/ppermute | solution.py:189
  87.3 19.7 %collective-permute-start.11 = (f32[2,8,1728]{2,1,0:T(8,128)}, f32[2,8,1728]{2,1,0:T(8,128)}, u32[]{:S(2)}, u32[]{:S(2)}) collective-permute-start(f32[2,8,1728]{2,1,0:T(8,128)} %get-tuple-element.19), channel_id=1, source_target_pairs={{0,4},{1,5},{2,6},{3,7},{4,8},{5,9},{6,10},{7,11},{8,12},{9,13},{1... | collective-permute-start | bytes 331784 | tf_op jit(solution)/shard_map/ppermute | solution.py:189
  90.1 20.4 %collective-permute-start.12 = (f32[2,8,1728]{2,1,0:T(8,128)}, f32[2,8,1728]{2,1,0:T(8,128)}, u32[]{:S(2)}, u32[]{:S(2)}) collective-permute-start(f32[2,8,1728]{2,1,0:T(8,128)} %get-tuple-element.18), channel_id=1, source_target_pairs={{0,5},{1,6},{2,7},{3,8},{4,9},{5,10},{6,11},{7,12},{8,13},{9,14},{... | collective-permute-start | bytes 331784 | tf_op jit(solution)/shard_map/ppermute | solution.py:189
  95.2 22.0 %collective-permute-start.13 = (f32[2,8,1728]{2,1,0:T(8,128)}, f32[2,8,1728]{2,1,0:T(8,128)}, u32[]{:S(2)}, u32[]{:S(2)}) collective-permute-start(f32[2,8,1728]{2,1,0:T(8,128)} %get-tuple-element.17), channel_id=1, source_target_pairs={{0,6},{1,7},{2,8},{3,9},{4,10},{5,11},{6,12},{7,13},{8,14},{9,15},... | collective-permute-start | bytes 331784 | tf_op jit(solution)/shard_map/ppermute | solution.py:189
  97.3 109.2 %copy-start.7 = (bf16[1,2,64,1152]{3,2,1,0:T(8,128)(2,1)S(1)}, bf16[1,2,64,1152]{3,2,1,0:T(8,128)(2,1)}, u32[]{:S(2)}) copy-start(bf16[1,2,64,1152]{3,2,1,0:T(8,128)(2,1)} %copy-done.6) | copy-start | bytes 884740
  97.3 24.8 %collective-permute-start.14 = (f32[2,8,1728]{2,1,0:T(8,128)}, f32[2,8,1728]{2,1,0:T(8,128)}, u32[]{:S(2)}, u32[]{:S(2)}) collective-permute-start(f32[2,8,1728]{2,1,0:T(8,128)} %get-tuple-element.16), channel_id=1, source_target_pairs={{0,7},{1,8},{2,9},{3,10},{4,11},{5,12},{6,13},{7,14},{8,15},{9,0},... | collective-permute-start | bytes 331784 | tf_op jit(solution)/shard_map/ppermute | solution.py:189
  103.7 131.4 %copy-start.5 = (bf16[1,2,64,1152]{3,2,1,0:T(8,128)(2,1)S(1)}, bf16[1,2,64,1152]{3,2,1,0:T(8,128)(2,1)}, u32[]{:S(2)}) copy-start(bf16[1,2,64,1152]{3,2,1,0:T(8,128)(2,1)} %copy-done.4) | copy-start | bytes 884740
  103.8 20.3 %collective-permute-start.15 = (f32[2,8,1728]{2,1,0:T(8,128)}, f32[2,8,1728]{2,1,0:T(8,128)S(1)}, u32[]{:S(2)}, u32[]{:S(2)}) collective-permute-start(f32[2,8,1728]{2,1,0:T(8,128)} %get-tuple-element.15), channel_id=1, source_target_pairs={{0,8},{1,9},{2,10},{3,11},{4,12},{5,13},{6,14},{7,15},{8,0},{9,1},... | collective-permute-start | bytes 331784 | tf_op jit(solution)/shard_map/ppermute | solution.py:189
  107.1 20.5 %collective-permute-start.16 = (f32[2,8,1728]{2,1,0:T(8,128)}, f32[2,8,1728]{2,1,0:T(8,128)S(1)}, u32[]{:S(2)}, u32[]{:S(2)}) collective-permute-start(f32[2,8,1728]{2,1,0:T(8,128)} %get-tuple-element.14), channel_id=1, source_target_pairs={{0,9},{1,10},{2,11},{3,12},{4,13},{5,14},{6,15},{7,0},{8,1},{9,2},... | collective-permute-start | bytes 331784 | tf_op jit(solution)/shard_map/ppermute | solution.py:189
  110.5 19.0 %collective-permute-start.17 = (f32[2,8,1728]{2,1,0:T(8,128)}, f32[2,8,1728]{2,1,0:T(8,128)S(1)}, u32[]{:S(2)}, u32[]{:S(2)}) collective-permute-start(f32[2,8,1728]{2,1,0:T(8,128)} %get-tuple-element.13), channel_id=1, source_target_pairs={{0,10},{1,11},{2,12},{3,13},{4,14},{5,15},{6,0},{7,1},{8,2},{9,3},... | collective-permute-start | bytes 331784 | tf_op jit(solution)/shard_map/ppermute | solution.py:189
  117.2 18.2 %collective-permute-start.18 = (f32[2,8,1728]{2,1,0:T(8,128)}, f32[2,8,1728]{2,1,0:T(8,128)S(1)}, u32[]{:S(2)}, u32[]{:S(2)}) collective-permute-start(f32[2,8,1728]{2,1,0:T(8,128)} %get-tuple-element.12), channel_id=1, source_target_pairs={{0,11},{1,12},{2,13},{3,14},{4,15},{5,0},{6,1},{7,2},{8,3},{9,4},{... | collective-permute-start | bytes 331784 | tf_op jit(solution)/shard_map/ppermute | solution.py:189
  122.1 15.1 %collective-permute-start.19 = (f32[2,8,1728]{2,1,0:T(8,128)}, f32[2,8,1728]{2,1,0:T(8,128)S(1)}, u32[]{:S(2)}, u32[]{:S(2)}) collective-permute-start(f32[2,8,1728]{2,1,0:T(8,128)} %get-tuple-element.11), channel_id=1, source_target_pairs={{0,12},{1,13},{2,14},{3,15},{4,0},{5,1},{6,2},{7,3},{8,4},{9,5},{1... | collective-permute-start | bytes 331784 | tf_op jit(solution)/shard_map/ppermute | solution.py:189
  124.1 16.7 %collective-permute-start.20 = (f32[2,8,1728]{2,1,0:T(8,128)}, f32[2,8,1728]{2,1,0:T(8,128)S(1)}, u32[]{:S(2)}, u32[]{:S(2)}) collective-permute-start(f32[2,8,1728]{2,1,0:T(8,128)} %get-tuple-element.10), channel_id=1, source_target_pairs={{0,13},{1,14},{2,15},{3,0},{4,1},{5,2},{6,3},{7,4},{8,5},{9,6},{10... | collective-permute-start | bytes 331784 | tf_op jit(solution)/shard_map/ppermute | solution.py:189
  127.5 13.3 %collective-permute-start.21 = (f32[2,8,1728]{2,1,0:T(8,128)}, f32[2,8,1728]{2,1,0:T(8,128)S(1)}, u32[]{:S(2)}, u32[]{:S(2)}) collective-permute-start(f32[2,8,1728]{2,1,0:T(8,128)} %get-tuple-element.9), channel_id=1, source_target_pairs={{0,14},{1,15},{2,0},{3,1},{4,2},{5,3},{6,4},{7,5},{8,6},{9,7},{10,... | collective-permute-start | bytes 331784 | tf_op jit(solution)/shard_map/ppermute | solution.py:189
  129.5 11.3 %collective-permute-start.22 = (f32[2,8,1728]{2,1,0:T(8,128)}, f32[2,8,1728]{2,1,0:T(8,128)S(1)}, u32[]{:S(2)}, u32[]{:S(2)}) collective-permute-start(f32[2,8,1728]{2,1,0:T(8,128)} %get-tuple-element.8), channel_id=1, source_target_pairs={{0,15},{1,0},{2,1},{3,2},{4,3},{5,4},{6,5},{7,6},{8,7},{9,8},{10,9... | collective-permute-start | bytes 331784 | tf_op jit(solution)/shard_map/ppermute | solution.py:189
  135.3 8.8 %collective-permute-start.8 = (f32[2,8,1728]{2,1,0:T(8,128)S(1)}, f32[2,8,1728]{2,1,0:T(8,128)S(1)}, u32[]{:S(2)}, u32[]{:S(2)}) collective-permute-start(f32[2,8,1728]{2,1,0:T(8,128)S(1)} %get-tuple-element.7), channel_id=1, source_target_pairs={{0,1},{1,2},{2,3},{3,4},{4,5},{5,6},{6,7},{7,8},{8,9},{9,10},{10,1... | collective-permute-start | bytes 331784 | tf_op jit(solution)/shard_map/ppermute | solution.py:189
  137.3 9.1 %collective-permute-start.9 = (f32[2,8,1728]{2,1,0:T(8,128)S(1)}, f32[2,8,1728]{2,1,0:T(8,128)S(1)}, u32[]{:S(2)}, u32[]{:S(2)}) collective-permute-start(f32[2,8,1728]{2,1,0:T(8,128)S(1)} %get-tuple-element.21), channel_id=1, source_target_pairs={{0,2},{1,3},{2,4},{3,5},{4,6},{5,7},{6,8},{7,9},{8,10},{9,11},{10,... | collective-permute-start | bytes 331784 | tf_op jit(solution)/shard_map/ppermute | solution.py:189
  147.7 28.4 %collective-permute-start.23 = (f32[2,1728]{1,0:T(2,128)S(1)}, f32[2,1728]{1,0:T(2,128)S(1)}, u32[]{:S(2)}, u32[]{:S(2)}) collective-permute-start(f32[2,1728]{1,0:T(2,128)S(1)} %bitcast.339), channel_id=1, source_target_pairs={{0,16},{16,32},{32,48},{48,64},{64,80},{80,96},{96,112},{112,0},{1... | collective-permute-start | bytes 41480 | tf_op jit(solution)/shard_map/ppermute | solution.py:189
  152.1 29.3 %collective-permute-start.24 = (f32[2,1728]{1,0:T(2,128)S(1)}, f32[2,1728]{1,0:T(2,128)S(1)}, u32[]{:S(2)}, u32[]{:S(2)}) collective-permute-start(f32[2,1728]{1,0:T(2,128)S(1)} %bitcast.338), channel_id=1, source_target_pairs={{0,32},{16,48},{32,64},{48,80},{64,96},{80,112},{96,0},{112,16},{1... | collective-permute-start | bytes 41480 | tf_op jit(solution)/shard_map/ppermute | solution.py:189
  159.2 27.1 %collective-permute-start.25 = (f32[2,1728]{1,0:T(2,128)S(1)}, f32[2,1728]{1,0:T(2,128)S(1)}, u32[]{:S(2)}, u32[]{:S(2)}) collective-permute-start(f32[2,1728]{1,0:T(2,128)S(1)} %bitcast.333), channel_id=1, source_target_pairs={{0,48},{16,64},{32,80},{48,96},{64,112},{80,0},{96,16},{112,32},{1... | collective-permute-start | bytes 41480 | tf_op jit(solution)/shard_map/ppermute | solution.py:189
  165.1 21.2 %collective-permute-start.26 = (f32[2,1728]{1,0:T(2,128)S(1)}, f32[2,1728]{1,0:T(2,128)S(1)}, u32[]{:S(2)}, u32[]{:S(2)}) collective-permute-start(f32[2,1728]{1,0:T(2,128)S(1)} %bitcast.334), channel_id=1, source_target_pairs={{0,64},{16,80},{32,96},{48,112},{64,0},{80,16},{96,32},{112,48},{1... | collective-permute-start | bytes 41480 | tf_op jit(solution)/shard_map/ppermute | solution.py:189
  168.2 18.1 %collective-permute-start.27 = (f32[2,1728]{1,0:T(2,128)S(1)}, f32[2,1728]{1,0:T(2,128)S(1)}, u32[]{:S(2)}, u32[]{:S(2)}) collective-permute-start(f32[2,1728]{1,0:T(2,128)S(1)} %bitcast.335), channel_id=1, source_target_pairs={{0,80},{16,96},{32,112},{48,0},{64,16},{80,32},{96,48},{112,64},{1... | collective-permute-start | bytes 41480 | tf_op jit(solution)/shard_map/ppermute | solution.py:189
  176.1 10.2 %collective-permute-start.28 = (f32[2,1728]{1,0:T(2,128)S(1)}, f32[2,1728]{1,0:T(2,128)S(1)}, u32[]{:S(2)}, u32[]{:S(2)}) collective-permute-start(f32[2,1728]{1,0:T(2,128)S(1)} %bitcast.337), channel_id=1, source_target_pairs={{0,96},{16,112},{32,0},{48,16},{64,32},{80,48},{96,64},{112,80},{1... | collective-permute-start | bytes 41480 | tf_op jit(solution)/shard_map/ppermute | solution.py:189
  181.4 6.2 %collective-permute-start.29 = (f32[2,1728]{1,0:T(2,128)S(1)}, f32[2,1728]{1,0:T(2,128)S(1)}, u32[]{:S(2)}, u32[]{:S(2)}) collective-permute-start(f32[2,1728]{1,0:T(2,128)S(1)} %bitcast.336), channel_id=1, source_target_pairs={{0,112},{16,0},{32,16},{48,32},{64,48},{80,64},{96,80},{112,96},{1... | collective-permute-start | bytes 41480 | tf_op jit(solution)/shard_map/ppermute | solution.py:189
  187.7 14.6 %collective-permute-start.30 = (f32[1728]{0:T(1024)S(1)}, f32[1728]{0:T(1024)S(1)}, u32[]{:S(2)}, u32[]{:S(2)}) collective-permute-start(f32[1728]{0:T(1024)S(1)} %get-tuple-element.3), channel_id=1, source_target_pairs={{0,256},{128,384},{256,0},{384,128},{1,257},{129,385},{257,1},{385... | collective-permute-start | bytes 20744 | tf_op jit(solution)/shard_map/ppermute | solution.py:180
  202.3 26.6 %collective-permute-start.31 = (bf16[1728]{0:T(1024)(128)(2,1)S(1)}, bf16[1728]{0:T(1024)(128)(2,1)S(1)}, u32[]{:S(2)}, u32[]{:S(2)}) collective-permute-start(bf16[1728]{0:T(1024)(128)(2,1)S(1)} %add_convert_fusion), channel_id=1, source_target_pairs={{0,16},{16,32},{32,48},{48,64},{64,80},{80,96},{96,112},{112,0},{1... | collective-permute-start | bytes 10376 | tf_op jit(solution)/shard_map/ppermute | solution.py:213
  204.3 26.6 %collective-permute-start.32 = (bf16[1728]{0:T(1024)(128)(2,1)S(1)}, bf16[1728]{0:T(1024)(128)(2,1)S(1)}, u32[]{:S(2)}, u32[]{:S(2)}) collective-permute-start(bf16[1728]{0:T(1024)(128)(2,1)S(1)} %add_convert_fusion), channel_id=1, source_target_pairs={{0,32},{16,48},{32,64},{48,80},{64,96},{80,112},{96,0},{112,16},{1... | collective-permute-start | bytes 10376 | tf_op jit(solution)/shard_map/ppermute | solution.py:213
  207.3 29.5 %collective-permute-start.33 = (bf16[1728]{0:T(1024)(128)(2,1)S(1)}, bf16[1728]{0:T(1024)(128)(2,1)S(1)}, u32[]{:S(2)}, u32[]{:S(2)}) collective-permute-start(bf16[1728]{0:T(1024)(128)(2,1)S(1)} %add_convert_fusion), channel_id=1, source_target_pairs={{0,48},{16,64},{32,80},{48,96},{64,112},{80,0},{96,16},{112,32},{1... | collective-permute-start | bytes 10376 | tf_op jit(solution)/shard_map/ppermute | solution.py:213
  213.4 23.3 %collective-permute-start.34 = (bf16[1728]{0:T(1024)(128)(2,1)S(1)}, bf16[1728]{0:T(1024)(128)(2,1)S(1)}, u32[]{:S(2)}, u32[]{:S(2)}) collective-permute-start(bf16[1728]{0:T(1024)(128)(2,1)S(1)} %add_convert_fusion), channel_id=1, source_target_pairs={{0,64},{16,80},{32,96},{48,112},{64,0},{80,16},{96,32},{112,48},{1... | collective-permute-start | bytes 10376 | tf_op jit(solution)/shard_map/ppermute | solution.py:213
  221.1 15.7 %collective-permute-start.35 = (bf16[1728]{0:T(1024)(128)(2,1)S(1)}, bf16[1728]{0:T(1024)(128)(2,1)S(1)}, u32[]{:S(2)}, u32[]{:S(2)}) collective-permute-start(bf16[1728]{0:T(1024)(128)(2,1)S(1)} %add_convert_fusion), channel_id=1, source_target_pairs={{0,80},{16,96},{32,112},{48,0},{64,16},{80,32},{96,48},{112,64},{1... | collective-permute-start | bytes 10376 | tf_op jit(solution)/shard_map/ppermute | solution.py:213
  229.0 7.9 %collective-permute-start.36 = (bf16[1728]{0:T(1024)(128)(2,1)S(1)}, bf16[1728]{0:T(1024)(128)(2,1)S(1)}, u32[]{:S(2)}, u32[]{:S(2)}) collective-permute-start(bf16[1728]{0:T(1024)(128)(2,1)S(1)} %add_convert_fusion), channel_id=1, source_target_pairs={{0,96},{16,112},{32,0},{48,16},{64,32},{80,48},{96,64},{112,80},{1... | collective-permute-start | bytes 10376 | tf_op jit(solution)/shard_map/ppermute | solution.py:213
  230.9 5.9 %collective-permute-start.37 = (bf16[1728]{0:T(1024)(128)(2,1)S(1)}, bf16[1728]{0:T(1024)(128)(2,1)S(1)}, u32[]{:S(2)}, u32[]{:S(2)}) collective-permute-start(bf16[1728]{0:T(1024)(128)(2,1)S(1)} %add_convert_fusion), channel_id=1, source_target_pairs={{0,112},{16,0},{32,16},{48,32},{64,48},{80,64},{96,80},{112,96},{1... | collective-permute-start | bytes 10376 | tf_op jit(solution)/shard_map/ppermute | solution.py:213
  237.5 18.4 %collective-permute-start.38 = (bf16[8,1728]{1,0:T(8,128)(2,1)S(1)}, bf16[8,1728]{1,0:T(8,128)(2,1)S(1)}, u32[]{:S(2)}, u32[]{:S(2)}) collective-permute-start(bf16[8,1728]{1,0:T(8,128)(2,1)S(1)} %gather_fusion), channel_id=1, source_target_pairs={{0,1},{1,2},{2,3},{3,4},{4,5},{5,6},{6,7},{7,8},{8,9},{9,10},{10,1... | collective-permute-start | bytes 82952 | tf_op jit(solution)/shard_map/ppermute | solution.py:213
  240.0 21.3 %collective-permute-start.39 = (bf16[8,1728]{1,0:T(8,128)(2,1)S(1)}, bf16[8,1728]{1,0:T(8,128)(2,1)S(1)}, u32[]{:S(2)}, u32[]{:S(2)}) collective-permute-start(bf16[8,1728]{1,0:T(8,128)(2,1)S(1)} %gather_fusion), channel_id=1, source_target_pairs={{0,2},{1,3},{2,4},{3,5},{4,6},{5,7},{6,8},{7,9},{8,10},{9,11},{10,... | collective-permute-start | bytes 82952 | tf_op jit(solution)/shard_map/ppermute | solution.py:213
  245.5 19.7 %collective-permute-start.40 = (bf16[8,1728]{1,0:T(8,128)(2,1)S(1)}, bf16[8,1728]{1,0:T(8,128)(2,1)S(1)}, u32[]{:S(2)}, u32[]{:S(2)}) collective-permute-start(bf16[8,1728]{1,0:T(8,128)(2,1)S(1)} %gather_fusion), channel_id=1, source_target_pairs={{0,3},{1,4},{2,5},{3,6},{4,7},{5,8},{6,9},{7,10},{8,11},{9,12},{10... | collective-permute-start | bytes 82952 | tf_op jit(solution)/shard_map/ppermute | solution.py:213
  249.7 19.1 %collective-permute-start.41 = (bf16[8,1728]{1,0:T(8,128)(2,1)S(1)}, bf16[8,1728]{1,0:T(8,128)(2,1)S(1)}, u32[]{:S(2)}, u32[]{:S(2)}) collective-permute-start(bf16[8,1728]{1,0:T(8,128)(2,1)S(1)} %gather_fusion), channel_id=1, source_target_pairs={{0,4},{1,5},{2,6},{3,7},{4,8},{5,9},{6,10},{7,11},{8,12},{9,13},{1... | collective-permute-start | bytes 82952 | tf_op jit(solution)/shard_map/ppermute | solution.py:213
  252.5 19.8 %collective-permute-start.42 = (bf16[8,1728]{1,0:T(8,128)(2,1)S(1)}, bf16[8,1728]{1,0:T(8,128)(2,1)S(1)}, u32[]{:S(2)}, u32[]{:S(2)}) collective-permute-start(bf16[8,1728]{1,0:T(8,128)(2,1)S(1)} %gather_fusion), channel_id=1, source_target_pairs={{0,5},{1,6},{2,7},{3,8},{4,9},{5,10},{6,11},{7,12},{8,13},{9,14},{... | collective-permute-start | bytes 82952 | tf_op jit(solution)/shard_map/ppermute | solution.py:213
  255.9 21.8 %collective-permute-start.43 = (bf16[8,1728]{1,0:T(8,128)(2,1)S(1)}, bf16[8,1728]{1,0:T(8,128)(2,1)S(1)}, u32[]{:S(2)}, u32[]{:S(2)}) collective-permute-start(bf16[8,1728]{1,0:T(8,128)(2,1)S(1)} %gather_fusion), channel_id=1, source_target_pairs={{0,6},{1,7},{2,8},{3,9},{4,10},{5,11},{6,12},{7,13},{8,14},{9,15},... | collective-permute-start | bytes 82952 | tf_op jit(solution)/shard_map/ppermute | solution.py:213
  261.4 19.9 %collective-permute-start.44 = (bf16[8,1728]{1,0:T(8,128)(2,1)S(1)}, bf16[8,1728]{1,0:T(8,128)(2,1)S(1)}, u32[]{:S(2)}, u32[]{:S(2)}) collective-permute-start(bf16[8,1728]{1,0:T(8,128)(2,1)S(1)} %gather_fusion), channel_id=1, source_target_pairs={{0,7},{1,8},{2,9},{3,10},{4,11},{5,12},{6,13},{7,14},{8,15},{9,0},... | collective-permute-start | bytes 82952 | tf_op jit(solution)/shard_map/ppermute | solution.py:213
  265.2 19.7 %collective-permute-start.45 = (bf16[8,1728]{1,0:T(8,128)(2,1)S(1)}, bf16[8,1728]{1,0:T(8,128)(2,1)S(1)}, u32[]{:S(2)}, u32[]{:S(2)}) collective-permute-start(bf16[8,1728]{1,0:T(8,128)(2,1)S(1)} %gather_fusion), channel_id=1, source_target_pairs={{0,8},{1,9},{2,10},{3,11},{4,12},{5,13},{6,14},{7,15},{8,0},{9,1},... | collective-permute-start | bytes 82952 | tf_op jit(solution)/shard_map/ppermute | solution.py:213
  268.8 18.0 %collective-permute-start.46 = (bf16[8,1728]{1,0:T(8,128)(2,1)S(1)}, bf16[8,1728]{1,0:T(8,128)(2,1)S(1)}, u32[]{:S(2)}, u32[]{:S(2)}) collective-permute-start(bf16[8,1728]{1,0:T(8,128)(2,1)S(1)} %gather_fusion), channel_id=1, source_target_pairs={{0,9},{1,10},{2,11},{3,12},{4,13},{5,14},{6,15},{7,0},{8,1},{9,2},... | collective-permute-start | bytes 82952 | tf_op jit(solution)/shard_map/ppermute | solution.py:213
  272.2 18.7 %collective-permute-start.47 = (bf16[8,1728]{1,0:T(8,128)(2,1)S(1)}, bf16[8,1728]{1,0:T(8,128)(2,1)S(1)}, u32[]{:S(2)}, u32[]{:S(2)}) collective-permute-start(bf16[8,1728]{1,0:T(8,128)(2,1)S(1)} %gather_fusion), channel_id=1, source_target_pairs={{0,10},{1,11},{2,12},{3,13},{4,14},{5,15},{6,0},{7,1},{8,2},{9,3},... | collective-permute-start | bytes 82952 | tf_op jit(solution)/shard_map/ppermute | solution.py:213
  277.7 18.8 %collective-permute-start.48 = (bf16[8,1728]{1,0:T(8,128)(2,1)S(1)}, bf16[8,1728]{1,0:T(8,128)(2,1)S(1)}, u32[]{:S(2)}, u32[]{:S(2)}) collective-permute-start(bf16[8,1728]{1,0:T(8,128)(2,1)S(1)} %gather_fusion), channel_id=1, source_target_pairs={{0,11},{1,12},{2,13},{3,14},{4,15},{5,0},{6,1},{7,2},{8,3},{9,4},{... | collective-permute-start | bytes 82952 | tf_op jit(solution)/shard_map/ppermute | solution.py:213
  281.2 15.3 %collective-permute-start.49 = (bf16[8,1728]{1,0:T(8,128)(2,1)S(1)}, bf16[8,1728]{1,0:T(8,128)(2,1)S(1)}, u32[]{:S(2)}, u32[]{:S(2)}) collective-permute-start(bf16[8,1728]{1,0:T(8,128)(2,1)S(1)} %gather_fusion), channel_id=1, source_target_pairs={{0,12},{1,13},{2,14},{3,15},{4,0},{5,1},{6,2},{7,3},{8,4},{9,5},{1... | collective-permute-start | bytes 82952 | tf_op jit(solution)/shard_map/ppermute | solution.py:213
  284.9 11.6 %collective-permute-start.50 = (bf16[8,1728]{1,0:T(8,128)(2,1)S(1)}, bf16[8,1728]{1,0:T(8,128)(2,1)S(1)}, u32[]{:S(2)}, u32[]{:S(2)}) collective-permute-start(bf16[8,1728]{1,0:T(8,128)(2,1)S(1)} %gather_fusion), channel_id=1, source_target_pairs={{0,13},{1,14},{2,15},{3,0},{4,1},{5,2},{6,3},{7,4},{8,5},{9,6},{10... | collective-permute-start | bytes 82952 | tf_op jit(solution)/shard_map/ppermute | solution.py:213
  286.9 9.7 %collective-permute-start.51 = (bf16[8,1728]{1,0:T(8,128)(2,1)S(1)}, bf16[8,1728]{1,0:T(8,128)(2,1)S(1)}, u32[]{:S(2)}, u32[]{:S(2)}) collective-permute-start(bf16[8,1728]{1,0:T(8,128)(2,1)S(1)} %gather_fusion), channel_id=1, source_target_pairs={{0,14},{1,15},{2,0},{3,1},{4,2},{5,3},{6,4},{7,5},{8,6},{9,7},{10,... | collective-permute-start | bytes 82952 | tf_op jit(solution)/shard_map/ppermute | solution.py:213
  290.9 7.1 %collective-permute-start.52 = (bf16[8,1728]{1,0:T(8,128)(2,1)S(1)}, bf16[8,1728]{1,0:T(8,128)(2,1)S(1)}, u32[]{:S(2)}, u32[]{:S(2)}) collective-permute-start(bf16[8,1728]{1,0:T(8,128)(2,1)S(1)} %gather_fusion), channel_id=1, source_target_pairs={{0,15},{1,0},{2,1},{3,2},{4,3},{5,4},{6,5},{7,6},{8,7},{9,8},{10,9... | collective-permute-start | bytes 82952 | tf_op jit(solution)/shard_map/ppermute | solution.py:213
  (1 other events, 0.7 us)

commit v3 on v1

--- a/solution.py
+++ b/solution.py
@@ -163,19 +163,58 @@
         return jnp.transpose(term, (1, 0, 2, 3)).reshape(quarters, -1)
 
     stacked = jnp.concatenate([by_quarter(first_local), by_quarter(down_local)], axis=1)
-    rows_n, frames_n = lax.axis_size("height"), lax.axis_size("tm")
-    piece = stacked.reshape(quarters, rows_n, frames_n, -1)
-    piece = lax.psum_scatter(piece, "height", scatter_dimension=1, tiled=True)
-    piece = lax.psum_scatter(piece, "tm", scatter_dimension=2, tiled=True)
-    piece = lax.psum_scatter(piece, "dp", scatter_dimension=0, tiled=True)
-    piece = piece.astype(jnp.bfloat16)
-    piece = lax.all_gather(piece, "tm", axis=2, tiled=True)
-    gathered = lax.all_gather(piece, "height", axis=1, tiled=True).reshape(-1)
+    gathered = reduce_gradients(stacked).reshape(-1)
     half = gathered.shape[0] // 2
     kernel_shape = (3, 3, 3, share, conv_first.shape[-1])
     summed_first = gathered[:half].reshape(kernel_shape)
     summed_down = gathered[half:].reshape(kernel_shape)
     return (encoded[None], summed_first, summed_down)
+
+
+def swap(value, axis, bit):
+    return lax.ppermute(value, axis, [(i, i ^ bit) for i in range(lax.axis_size(axis))])
+
+
+def bits_of(count):
+    return [1 << k for k in range(count.bit_length() - 1)]
+
+
+def split_bit(blocks, names, name, high):
+    place = names.index(name)
+    mine = lax.dynamic_index_in_dim(blocks, high, place, keepdims=False)
+    other = lax.dynamic_index_in_dim(blocks, 1 - high, place, keepdims=False)
+    return mine, other, names[:place] + names[place + 1 :]
+
+
+def reduce_gradients(stacked):
+    dp_bits = bits_of(lax.axis_size("dp"))
+    row_bits = bits_of(lax.axis_size("height"))
+    frame_bits = bits_of(lax.axis_size("tm"))
+    names = [("dp", bit) for bit in reversed(dp_bits)] + [("height", bit) for bit in reversed(row_bits)]
+    blocks = stacked.reshape((2,) * len(names) + (-1,))
+    order = [("dp", bit) for bit in dp_bits[:-1]]
+    near = row_bits[0::2] + row_bits[1::2]
+    order += [("height", bit) for bit in near]
+    for axis, bit in order:
+        high = (lax.axis_index(axis) // bit) % 2
+        mine, other, names = split_bit(blocks, names, (axis, bit), high)
+        blocks = mine + swap(other, axis, bit)
+    for bit in frame_bits:
+        blocks = blocks + swap(blocks, "tm", bit)
+    far = dp_bits[-1]
+    high = (lax.axis_index("dp") // far) % 2
+    mine, other, names = split_bit(blocks, names, ("dp", far), high)
+    piece = (mine + swap(other, "dp", far)).astype(jnp.bfloat16)
+    present = []
+    for bit in reversed(near):
+        other = swap(piece, "height", bit)
+        high = (lax.axis_index("height") // bit) % 2
+        place = sum(1 for held in present if held > bit)
+        low_first = jnp.stack([piece, other], axis=place)
+        high_first = jnp.stack([other, piece], axis=place)
+        piece = jnp.where(high == 0, low_first, high_first)
+        present.append(bit)
+    return piece
 
 
 def solution(mesh):

time: 462 us -> 229 us (0.50)
  waiting for transfers between devices: 255 us -> 83.5 us
  blocking collectives: 103 us -> 0 us
  starting transfers between devices: 24.5 us -> 85.1 us
  local copies, waits for them, and re-layouts: 43.2 us -> 28.3 us
  between operations: 16.9 us -> 4.24 us
  other arithmetic: 8.16 us -> 17 us
    unnamed x4 -> x0, waiting for transfers between devices: 245 us -> none
    ppermute x0 -> x13, waiting for transfers between devices: none -> 72.7 us  [swap(): lax.ppermute(value, axis, [(i, i ^ bit) for i in range(lax.axis_size(axis...]
    all_gather x2 -> x0, blocking collectives: 70.4 us -> none  [the longest x1 46.8 us: body(): piece = lax.all_gather(piece, 'tm', axis=2, tiled=True)]
    ppermute x0 -> x13, starting transfers between devices: none -> 60.9 us  [swap(): lax.ppermute(value, axis, [(i, i ^ bit) for i in range(lax.axis_size(axis...]
    unnamed x1 -> x0, blocking collectives: 32.2 us -> none
    unnamed x66 -> x78, local copies, waits for them, and re-layouts: 17 us -> 6.89 us
    slice x27, local copies, waits for them, and re-layouts: 9.5 us -> 3.37 us  [unfold(): padded[:, tap_row:tap_row + stride * (out_rows - 1) + 1:stride, tap_col:t...]
    reshape x0 -> x1, local copies, waits for them, and re-layouts: none -> 5.63 us  [reduce_gradients(): blocks = stacked.reshape((2,) * len(names) + (-1,))]
  transfers between devices with their start and end apart: 9 -> 20, of which waited for: 5 -> 16; matrix products, arithmetic and copies ran while one was open for 4% -> 7% of each run, Pallas kernels for 0% -> 0%
where the time goes in v3:
time: 229 us; the launch traced here: 228 us
  starting transfers between devices  85.1 us (37%)
  waiting for transfers between devices  83.5 us (36%)
  local copies, waits for them, and re-layouts  28.3 us (12%)
  other arithmetic  17 us (7%)
  matrix products  10 us (4%)
  between operations  4.24 us (2%)
    ppermute x13, waiting for transfers between devices, swap(): lax.ppermute(value, axis, [(i, i ^ bit) for i in range(lax.axis_size(axis...  72.7 us
    ppermute x13, starting transfers between devices, swap(): lax.ppermute(value, axis, [(i, i ^ bit) for i in range(lax.axis_size(axis...  60.9 us
    ppermute x5, starting transfers between devices, shifted(): lax.ppermute(value, axis, [(source, source + steps) for source in range(l...  16.3 us
    ppermute x5, waiting for transfers between devices, shifted(): lax.ppermute(value, axis, [(source, source + steps) for source in range(l...  10.8 us
    unnamed x78, local copies, waits for them, and re-layouts  6.89 us
    concatenate x1, other arithmetic, body(): jnp.concatenate([by_quarter(first_local), by_quarter(down_local)], axis=1)  6.24 us
    reshape x1, local copies, waits for them, and re-layouts, reduce_gradients(): blocks = stacked.reshape((2,) * len(names) + (-1,))  5.63 us
    dot_general x6, matrix products, conv_layer(): jnp.dot(columns, kernel, preferred_element_type=jnp.float32)  5.63 us
  transfers between devices with their start and end apart: 20, of which 16 were waited for; matrix products, arithmetic and copies ran while one was open for 7% of the time, Pallas kernels for 0%

profile of v3, /device:TPU:6, one launch (start us, length us, event | category | flops | bytes accessed | tf_op | source)
XLA Modules:
  0.0 228.1 jit_solution(15863780284797087934)
XLA Ops:
  0.6 0.9 fusion.91
  1.6 3.5 %collective-permute-start = (bf16[2,1,128,128]{3,2,1,0:T(8,128)(2,1)S(1)}, bf16[2,1,128,128]{3,2,1,0:T(8,128)(2,1)S(1)}, u32[]{:S(2)}, u32[]{:S(2)}) collective-permute-start(bf16[2,1,128,128]{3,2,1,0:T(8,128)(2,1)S(1)} %get-tuple-element.23), channel_id=1, source_target_pairs={{0,1},{1,2},{2,3},{3,4},{4,5},{5,6},{6,7},{7,8},{8,9},{9,10},{10,1... | collective-permute-start | bytes 196616 | tf_op jit(solution)/shard_map/ppermute | solution.py:17
  5.1 4.5 %collective-permute-start.1 = (bf16[2,1,128,128]{3,2,1,0:T(8,128)(2,1)S(1)}, bf16[2,1,128,128]{3,2,1,0:T(8,128)(2,1)S(1)}, u32[]{:S(2)}, u32[]{:S(2)}) collective-permute-start(bf16[2,1,128,128]{3,2,1,0:T(8,128)(2,1)S(1)} %get-tuple-element.24), channel_id=1, source_target_pairs={{1,0},{2,1},{3,2},{4,3},{5,4},{6,5},{7,6},{8,7},{9,8},{10,9},{11,1... | collective-permute-start | bytes 196616 | tf_op jit(solution)/shard_map/ppermute | solution.py:19
  9.5 0.8 fusion.60
  10.3 3.1 %collective-permute-start.5 = (bf16[1,1,64,128]{3,2,1,0:T(8,128)(2,1)S(1)}, bf16[1,1,64,128]{3,2,1,0:T(8,128)(2,1)S(1)}, u32[]{:S(2)}, u32[]{:S(2)}) collective-permute-start(bf16[1,1,64,128]{3,2,1,0:T(8,128)(2,1)S(1)} %slice.452), channel_id=1, source_target_pairs={{1,0},{2,1},{3,2},{4,3},{5,4},{6,5},{7,6},{8,7},{9,8},{10,9},{11,1... | collective-permute-start | bytes 49160 | tf_op jit(solution)/shard_map/ppermute | solution.py:29
  13.4 0.8 reduce-window_clone.1
  14.3 0.7 subtract_bitcast_fusion
  15.3 1.3 fusion.88
  20.2 1.3 collective-permute-start.6
  21.6 4.6 %collective-permute-start.2 = (bf16[2,6,128,128]{3,2,1,0:T(8,128)(2,1)S(1)}, bf16[2,6,128,128]{3,2,1,0:T(8,128)(2,1)S(1)}, u32[]{:S(2)}, u32[]{:S(2)}) collective-permute-start(bf16[2,6,128,128]{3,2,1,0:T(8,128)(2,1)S(1)} %pad_maximum_fusion.4), channel_id=1, source_target_pairs={{0,16},{16,32},{32,48},{48,64},{64,80},{80,96},{96,112},{1,17},{17... | collective-permute-start | bytes 1179656 | tf_op jit(solution)/shard_map/ppermute | solution.py:29
  26.3 1.3 multiply_bitcast_fusion.1
  30.1 3.4 %collective-permute-done.2 = bf16[2,6,128,128]{3,2,1,0:T(8,128)(2,1)S(1)} collective-permute-done((bf16[2,6,128,128]{3,2,1,0:T(8,128)(2,1)S(1)}, bf16[2,6,128,128]{3,2,1,0:T(8,128)(2,1)S(1)}, u32[]{:S(2)}, u32[]{:S(2)}) %collective-permute-start.2) | collective-permute-done | bytes 393248 | tf_op jit(solution)/shard_map/ppermute | solution.py:29
  34.6 0.8 convolution_multiply_fusion.1
  36.3 0.8 fusion.1
  37.1 0.9 fusion.10
  38.0 0.9 convolution_bitcast_fusion.5
  38.9 0.9 convolution_bitcast_fusion.4
  39.8 0.9 convolution_bitcast_fusion.3
  40.6 2.8 %collective-permute-start.3 = (bf16[2,1,128,128]{3,2,1,0:T(8,128)(2,1)S(1)}, bf16[2,1,128,128]{3,2,1,0:T(8,128)(2,1)S(1)}, u32[]{:S(2)}, u32[]{:S(2)}) collective-permute-start(bf16[2,1,128,128]{3,2,1,0:T(8,128)(2,1)S(1)} %slice.447), channel_id=1, source_target_pairs={{0,1},{1,2},{2,3},{3,4},{4,5},{5,6},{6,7},{7,8},{8,9},{9,10},{10,1... | collective-permute-start | bytes 196616 | tf_op jit(solution)/shard_map/ppermute | solution.py:29
  43.7 1.1 copy.118
  44.9 4.1 %collective-permute-done.3 = bf16[2,1,128,128]{3,2,1,0:T(8,128)(2,1)S(1)} collective-permute-done((bf16[2,1,128,128]{3,2,1,0:T(8,128)(2,1)S(1)}, bf16[2,1,128,128]{3,2,1,0:T(8,128)(2,1)S(1)}, u32[]{:S(2)}, u32[]{:S(2)}) %collective-permute-start.3) | collective-permute-done | bytes 65568 | tf_op jit(solution)/shard_map/ppermute | solution.py:29
  50.2 4.6 %collective-permute-start.4 = (bf16[2,5,128,128]{3,2,1,0:T(8,128)(2,1)S(1)}, bf16[2,5,128,128]{3,2,1,0:T(8,128)(2,1)S(1)}, u32[]{:S(2)}, u32[]{:S(2)}) collective-permute-start(bf16[2,5,128,128]{3,2,1,0:T(8,128)(2,1)S(1)} %pad_maximum_fusion.3), channel_id=1, source_target_pairs={{0,16},{16,32},{32,48},{48,64},{64,80},{80,96},{96,112},{1,17},{17... | collective-permute-start | bytes 983048 | tf_op jit(solution)/shard_map/ppermute | solution.py:29
  55.0 0.7 copy-done.3
  56.0 3.3 %collective-permute-done.4 = bf16[2,5,128,128]{3,2,1,0:T(8,128)(2,1)S(1)} collective-permute-done((bf16[2,5,128,128]{3,2,1,0:T(8,128)(2,1)S(1)}, bf16[2,5,128,128]{3,2,1,0:T(8,128)(2,1)S(1)}, u32[]{:S(2)}, u32[]{:S(2)}) %collective-permute-start.4) | collective-permute-done | bytes 327712 | tf_op jit(solution)/shard_map/ppermute | solution.py:29
  63.7 1.1 copy.117
  64.8 6.2 %pad_maximum_fusion = f32[4,221184]{1,0:T(4,128)} fusion(f32[4,110592]{1,0:T(4,128)S(1)} %bitcast.214, f32[4,110592]{1,0:T(4,128)S(1)} %bitcast.213), kind=kLoop, calls=%fused_computation | loop fusion | flops 884736 | bytes 7077888 | tf_op jit(solution)/shard_map/concatenate | solution.py:165
  71.1 5.6 %reshape.508 = f32[2,2,2,2,2,2,13824]{6,5,4,3,2,1,0:T(2,128)S(1)} reshape(f32[4,221184]{1,0:T(4,128)} %pad_maximum_fusion) | data formatting | bytes 7077888 | tf_op jit(solution)/shard_map/reshape | solution.py:194
  76.7 1.4 dynamic-slice_bitcast_fusion
  78.1 2.1 collective-permute-start.7
  80.2 3.7 %collective-permute-done.7 = f32[2,2,2,2,2,13824]{5,4,3,2,1,0:T(2,128)} collective-permute-done((f32[2,2,2,2,2,13824]{5,4,3,2,1,0:T(2,128)}, f32[2,2,2,2,2,13824]{5,4,3,2,1,0:T(2,128)}, u32[]{:S(2)}, u32[]{:S(2)}) %collective-permute-start.7) | collective-permute-done | bytes 1769504 | tf_op jit(solution)/shard_map/ppermute | solution.py:175
  84.0 2.4 %bitcast_add_fusion = f32[2,2,2,2,2,13824]{5,4,3,2,1,0:T(2,128)S(1)} fusion(f32[2,2,2,2,2,13824]{5,4,3,2,1,0:T(2,128)} %collective-permute-done.7, f32[2,2,2,2,2,2,13824]{6,5,4,3,2,1,0:T(2,128)S(1)} %reshape.508, s32[]{:T(128)S(6)} %select_n.200), kind=kLoop, calls=%fused_computation.11 | loop fusion | flops 442368 | bytes 5308420 | tf_op jit(solution)/shard_map/add | solution.py:201
  86.4 1.6 constant_dynamic-slice_fusion.5
  88.5 1.9 collective-permute-start.8
  90.4 21.6 %collective-permute-done.8 = f32[2,2,2,2,13824]{4,3,2,1,0:T(2,128)S(1)} collective-permute-done((f32[2,2,2,2,13824]{4,3,2,1,0:T(2,128)S(1)}, f32[2,2,2,2,13824]{4,3,2,1,0:T(2,128)S(1)}, u32[]{:S(2)}, u32[]{:S(2)}) %collective-permute-start.8) | collective-permute-done | bytes 884768 | tf_op jit(solution)/shard_map/ppermute | solution.py:175
  112.0 0.6 bitcast_add_fusion.1
  112.7 2.4 %collective-permute-start.9 = (f32[2,2,2,13824]{3,2,1,0:T(2,128)S(1)}, f32[2,2,2,13824]{3,2,1,0:T(2,128)S(1)}, u32[]{:S(2)}, u32[]{:S(2)}) collective-permute-start(f32[2,2,2,13824]{3,2,1,0:T(2,128)S(1)} %dynamic-slice_bitcast_fusion.1), channel_id=1, source_target_pairs={{0,4},{1,5},{2,6},{3,7},{4,0},{5,1},{6,2},{7,3},{8,12},{9,13},{10,... | collective-permute-start | bytes 1327112 | tf_op jit(solution)/shard_map/ppermute | solution.py:175
  115.2 10.8 %collective-permute-done.9 = f32[2,2,2,13824]{3,2,1,0:T(2,128)S(1)} collective-permute-done((f32[2,2,2,13824]{3,2,1,0:T(2,128)S(1)}, f32[2,2,2,13824]{3,2,1,0:T(2,128)S(1)}, u32[]{:S(2)}, u32[]{:S(2)}) %collective-permute-start.9) | collective-permute-done | bytes 442400 | tf_op jit(solution)/shard_map/ppermute | solution.py:175
  126.8 1.9 collective-permute-start.10
  128.7 7.4 %collective-permute-done.10 = f32[2,2,13824]{2,1,0:T(2,128)S(1)} collective-permute-done((f32[2,2,13824]{2,1,0:T(2,128)S(1)}, f32[2,2,13824]{2,1,0:T(2,128)S(1)}, u32[]{:S(2)}, u32[]{:S(2)}) %collective-permute-start.10) | collective-permute-done | bytes 221216 | tf_op jit(solution)/shard_map/ppermute | solution.py:175
  136.5 3.0 %collective-permute-start.11 = (f32[2,13824]{1,0:T(2,128)S(1)}, f32[2,13824]{1,0:T(2,128)S(1)}, u32[]{:S(2)}, u32[]{:S(2)}) collective-permute-start(f32[2,13824]{1,0:T(2,128)S(1)} %bitcast.240), channel_id=1, source_target_pairs={{0,8},{1,9},{2,10},{3,11},{4,12},{5,13},{6,14},{7,15},{8,0},{9,1},... | collective-permute-start | bytes 331784 | tf_op jit(solution)/shard_map/ppermute | solution.py:175
  139.6 5.1 %collective-permute-done.11 = f32[2,13824]{1,0:T(2,128)S(1)} collective-permute-done((f32[2,13824]{1,0:T(2,128)S(1)}, f32[2,13824]{1,0:T(2,128)S(1)}, u32[]{:S(2)}, u32[]{:S(2)}) %collective-permute-start.11) | collective-permute-done | bytes 110624 | tf_op jit(solution)/shard_map/ppermute | solution.py:175
  144.8 4.5 %collective-permute-start.12 = (f32[2,13824]{1,0:T(2,128)S(1)}, f32[2,13824]{1,0:T(2,128)S(1)}, u32[]{:S(2)}, u32[]{:S(2)}) collective-permute-start(f32[2,13824]{1,0:T(2,128)S(1)} %bitcast_add_fusion.4), channel_id=1, source_target_pairs={{0,16},{16,0},{32,48},{48,32},{64,80},{80,64},{96,112},{112,96},{1... | collective-permute-start | bytes 331784 | tf_op jit(solution)/shard_map/ppermute | solution.py:175
  149.3 2.7 %collective-permute-done.12 = f32[2,13824]{1,0:T(2,128)S(1)} collective-permute-done((f32[2,13824]{1,0:T(2,128)S(1)}, f32[2,13824]{1,0:T(2,128)S(1)}, u32[]{:S(2)}, u32[]{:S(2)}) %collective-permute-start.12) | collective-permute-done | bytes 110624 | tf_op jit(solution)/shard_map/ppermute | solution.py:175
  152.1 7.3 %collective-permute-start.13 = (f32[2,13824]{1,0:T(2,128)S(1)}, f32[2,13824]{1,0:T(2,128)S(1)}, u32[]{:S(2)}, u32[]{:S(2)}) collective-permute-start(f32[2,13824]{1,0:T(2,128)S(1)} %add.195), channel_id=1, source_target_pairs={{0,32},{16,48},{32,0},{48,16},{64,96},{80,112},{96,64},{112,80},{1... | collective-permute-start | bytes 331784 | tf_op jit(solution)/shard_map/ppermute | solution.py:175
  159.5 2.5 %collective-permute-done.13 = f32[2,13824]{1,0:T(2,128)S(1)} collective-permute-done((f32[2,13824]{1,0:T(2,128)S(1)}, f32[2,13824]{1,0:T(2,128)S(1)}, u32[]{:S(2)}, u32[]{:S(2)}) %collective-permute-start.13) | collective-permute-done | bytes 110624 | tf_op jit(solution)/shard_map/ppermute | solution.py:175
  162.1 11.9 %collective-permute-start.14 = (f32[2,13824]{1,0:T(2,128)S(1)}, f32[2,13824]{1,0:T(2,128)S(1)}, u32[]{:S(2)}, u32[]{:S(2)}) collective-permute-start(f32[2,13824]{1,0:T(2,128)S(1)} %add.196), channel_id=1, source_target_pairs={{0,64},{16,80},{32,96},{48,112},{64,0},{80,16},{96,32},{112,48},{1... | collective-permute-start | bytes 331784 | tf_op jit(solution)/shard_map/ppermute | solution.py:175
  174.1 0.8 convolution_multiply_fusion.5
  174.9 3.3 %collective-permute-done.14 = f32[2,13824]{1,0:T(2,128)S(1)} collective-permute-done((f32[2,13824]{1,0:T(2,128)S(1)}, f32[2,13824]{1,0:T(2,128)S(1)}, u32[]{:S(2)}, u32[]{:S(2)}) %collective-permute-start.14) | collective-permute-done | bytes 110624 | tf_op jit(solution)/shard_map/ppermute | solution.py:175
  178.5 13.5 %collective-permute-start.15 = (f32[13824]{0:T(1024)S(1)}, f32[13824]{0:T(1024)S(1)}, u32[]{:S(2)}, u32[]{:S(2)}) collective-permute-start(f32[13824]{0:T(1024)S(1)} %get-tuple-element.3), channel_id=1, source_target_pairs={{0,256},{128,384},{256,0},{384,128},{1,257},{129,385},{257,1},{385... | collective-permute-start | bytes 165896 | tf_op jit(solution)/shard_map/ppermute | solution.py:175
  192.0 0.8 fusion.6
  192.9 1.4 collective-permute-done.15
  194.2 3.0 %collective-permute-start.16 = (bf16[13824]{0:T(1024)(128)(2,1)S(1)}, bf16[13824]{0:T(1024)(128)(2,1)S(1)}, u32[]{:S(2)}, u32[]{:S(2)}) collective-permute-start(bf16[13824]{0:T(1024)(128)(2,1)S(1)} %add_convert_fusion), channel_id=1, source_target_pairs={{0,8},{1,9},{2,10},{3,11},{4,12},{5,13},{6,14},{7,15},{8,0},{9,1},... | collective-permute-start | bytes 82952 | tf_op jit(solution)/shard_map/ppermute | solution.py:175
  197.3 1.5 fusion.8
  198.8 2.7 %collective-permute-done.16 = bf16[13824]{0:T(1024)(128)(2,1)S(1)} collective-permute-done((bf16[13824]{0:T(1024)(128)(2,1)S(1)}, bf16[13824]{0:T(1024)(128)(2,1)S(1)}, u32[]{:S(2)}, u32[]{:S(2)}) %collective-permute-start.16) | collective-permute-done | bytes 27680 | tf_op jit(solution)/shard_map/ppermute | solution.py:175
  201.8 2.6 %collective-permute-start.17 = (bf16[2,13824]{1,0:T(2,128)(2,1)S(1)}, bf16[2,13824]{1,0:T(2,128)(2,1)S(1)}, u32[]{:S(2)}, u32[]{:S(2)}) collective-permute-start(bf16[2,13824]{1,0:T(2,128)(2,1)S(1)} %broadcast_select_fusion.5), channel_id=1, source_target_pairs={{0,2},{1,3},{2,0},{3,1},{4,6},{5,7},{6,4},{7,5},{8,10},{9,11},{10,... | collective-permute-start | bytes 165896 | tf_op jit(solution)/shard_map/ppermute | solution.py:175
  205.0 4.4 %collective-permute-done.17 = bf16[2,13824]{1,0:T(2,128)(2,1)S(1)} collective-permute-done((bf16[2,13824]{1,0:T(2,128)(2,1)S(1)}, bf16[2,13824]{1,0:T(2,128)(2,1)S(1)}, u32[]{:S(2)}, u32[]{:S(2)}) %collective-permute-start.17) | collective-permute-done | bytes 55328 | tf_op jit(solution)/shard_map/ppermute | solution.py:175
  209.5 2.4 %collective-permute-start.18 = (bf16[2,2,13824]{2,0,1:T(2,128)(2,1)S(1)}, bf16[2,2,13824]{2,0,1:T(2,128)(2,1)S(1)}, u32[]{:S(2)}, u32[]{:S(2)}) collective-permute-start(bf16[2,2,13824]{2,0,1:T(2,128)(2,1)S(1)} %broadcast_select_fusion.3), channel_id=1, source_target_pairs={{0,4},{1,5},{2,6},{3,7},{4,0},{5,1},{6,2},{7,3},{8,12},{9,13},{10,... | collective-permute-start | bytes 331784 | tf_op jit(solution)/shard_map/ppermute | solution.py:175
  212.3 3.9 %collective-permute-done.18 = bf16[2,2,13824]{2,0,1:T(2,128)(2,1)S(1)} collective-permute-done((bf16[2,2,13824]{2,0,1:T(2,128)(2,1)S(1)}, bf16[2,2,13824]{2,0,1:T(2,128)(2,1)S(1)}, u32[]{:S(2)}, u32[]{:S(2)}) %collective-permute-start.18) | collective-permute-done | bytes 110624 | tf_op jit(solution)/shard_map/ppermute | solution.py:175
  216.5 4.2 %collective-permute-start.19 = (bf16[2,2,2,13824]{3,0,2,1:T(2,128)(2,1)S(1)}, bf16[2,2,2,13824]{3,0,2,1:T(2,128)(2,1)S(1)}, u32[]{:S(2)}, u32[]{:S(2)}) collective-permute-start(bf16[2,2,2,13824]{3,0,2,1:T(2,128)(2,1)S(1)} %broadcast_select_fusion.1), channel_id=1, source_target_pairs={{0,1},{1,0},{2,3},{3,2},{4,5},{5,4},{6,7},{7,6},{8,9},{9,8},{10,11... | collective-permute-start | bytes 663560 | tf_op jit(solution)/shard_map/ppermute | solution.py:175
  221.1 3.3 %collective-permute-done.19 = bf16[2,2,2,13824]{3,0,2,1:T(2,128)(2,1)S(1)} collective-permute-done((bf16[2,2,2,13824]{3,0,2,1:T(2,128)(2,1)S(1)}, bf16[2,2,2,13824]{3,0,2,1:T(2,128)(2,1)S(1)}, u32[]{:S(2)}, u32[]{:S(2)}) %collective-permute-start.19) | collective-permute-done | bytes 221216 | tf_op jit(solution)/shard_map/ppermute | solution.py:175
  224.7 0.6 broadcast_select_fusion
  225.4 0.6 fusion.89
  226.2 0.8 reshape.509
  227.3 0.8 reshape.510
  (190 shorter events, 17.6 us)
Async XLA Ops:
  0.6 20.9 %copy-start = (bf16[1,2,4,128,128]{4,3,2,1,0:T(8,128)(2,1)S(1)}, bf16[1,2,4,128,128]{4,3,2,1,0:T(8,128)(2,1)}, u32[]{:S(2)}) copy-start(bf16[1,2,4,128,128]{4,3,2,1,0:T(8,128)(2,1)} %param.5) | copy-start | bytes 786436
  1.6 19.9 %collective-permute-start = (bf16[2,1,128,128]{3,2,1,0:T(8,128)(2,1)S(1)}, bf16[2,1,128,128]{3,2,1,0:T(8,128)(2,1)S(1)}, u32[]{:S(2)}, u32[]{:S(2)}) collective-permute-start(bf16[2,1,128,128]{3,2,1,0:T(8,128)(2,1)S(1)} %get-tuple-element.23), channel_id=1, source_target_pairs={{0,1},{1,2},{2,3},{3,4},{4,5},{5,6},{6,7},{7,8},{8,9},{9,10},{10,1... | collective-permute-start | bytes 196616 | tf_op jit(solution)/shard_map/ppermute | solution.py:17
  5.1 16.4 %collective-permute-start.1 = (bf16[2,1,128,128]{3,2,1,0:T(8,128)(2,1)S(1)}, bf16[2,1,128,128]{3,2,1,0:T(8,128)(2,1)S(1)}, u32[]{:S(2)}, u32[]{:S(2)}) collective-permute-start(bf16[2,1,128,128]{3,2,1,0:T(8,128)(2,1)S(1)} %get-tuple-element.24), channel_id=1, source_target_pairs={{1,0},{2,1},{3,2},{4,3},{5,4},{6,5},{7,6},{8,7},{9,8},{10,9},{11,1... | collective-permute-start | bytes 196616 | tf_op jit(solution)/shard_map/ppermute | solution.py:19
  10.3 9.8 %collective-permute-start.5 = (bf16[1,1,64,128]{3,2,1,0:T(8,128)(2,1)S(1)}, bf16[1,1,64,128]{3,2,1,0:T(8,128)(2,1)S(1)}, u32[]{:S(2)}, u32[]{:S(2)}) collective-permute-start(bf16[1,1,64,128]{3,2,1,0:T(8,128)(2,1)S(1)} %slice.452), channel_id=1, source_target_pairs={{1,0},{2,1},{3,2},{4,3},{5,4},{6,5},{7,6},{8,7},{9,8},{10,9},{11,1... | collective-permute-start | bytes 49160 | tf_op jit(solution)/shard_map/ppermute | solution.py:29
  15.3 12.7 %copy-start.7 = (bf16[3,3,3,128,128]{4,3,2,1,0:T(8,128)(2,1)S(1)}, bf16[3,3,3,128,128]{4,3,2,1,0:T(8,128)(2,1)}, u32[]{:S(2)}) copy-start(bf16[3,3,3,128,128]{4,3,2,1,0:T(8,128)(2,1)} %param.8) | copy-start | bytes 2654212
  15.3 12.7 %copy-start.10 = (pred[8,18]{0,1:T(8,128)(4,1)S(1)}, pred[8,18]{0,1:T(8,128)(4,1)}, u32[]{:S(2)}) copy-start(pred[8,18]{0,1:T(8,128)(4,1)} %constant.203) | copy-start | bytes 436
  20.2 6.1 %collective-permute-start.6 = (bf16[1,3,64,128]{3,2,1,0:T(8,128)(2,1)S(1)}, bf16[1,3,64,128]{3,2,1,0:T(8,128)(2,1)S(1)}, u32[]{:S(2)}, u32[]{:S(2)}) collective-permute-start(bf16[1,3,64,128]{3,2,1,0:T(8,128)(2,1)S(1)} %pad_maximum_fusion.8), channel_id=1, source_target_pairs={{16,0},{32,16},{48,32},{64,48},{80,64},{96,80},{112,96},{17,1},{33... | collective-permute-start | bytes 147464 | tf_op jit(solution)/shard_map/ppermute | solution.py:29
  21.6 12.0 %collective-permute-start.2 = (bf16[2,6,128,128]{3,2,1,0:T(8,128)(2,1)S(1)}, bf16[2,6,128,128]{3,2,1,0:T(8,128)(2,1)S(1)}, u32[]{:S(2)}, u32[]{:S(2)}) collective-permute-start(bf16[2,6,128,128]{3,2,1,0:T(8,128)(2,1)S(1)} %pad_maximum_fusion.4), channel_id=1, source_target_pairs={{0,16},{16,32},{32,48},{48,64},{64,80},{80,96},{96,112},{1,17},{17... | collective-permute-start | bytes 1179656 | tf_op jit(solution)/shard_map/ppermute | solution.py:29
  40.6 8.3 %collective-permute-start.3 = (bf16[2,1,128,128]{3,2,1,0:T(8,128)(2,1)S(1)}, bf16[2,1,128,128]{3,2,1,0:T(8,128)(2,1)S(1)}, u32[]{:S(2)}, u32[]{:S(2)}) collective-permute-start(bf16[2,1,128,128]{3,2,1,0:T(8,128)(2,1)S(1)} %slice.447), channel_id=1, source_target_pairs={{0,1},{1,2},{2,3},{3,4},{4,5},{5,6},{6,7},{7,8},{8,9},{9,10},{10,1... | collective-permute-start | bytes 196616 | tf_op jit(solution)/shard_map/ppermute | solution.py:29
  43.7 12.0 %copy-start.9 = (bf16[1,1,2,64,128]{4,3,2,1,0:T(8,128)(2,1)S(1)}, bf16[1,1,2,64,128]{4,3,2,1,0:T(8,128)(2,1)}, u32[]{:S(2)}) copy-start(bf16[1,1,2,64,128]{4,3,2,1,0:T(8,128)(2,1)} %param.9) | copy-start | bytes 98308
  50.2 9.0 %collective-permute-start.4 = (bf16[2,5,128,128]{3,2,1,0:T(8,128)(2,1)S(1)}, bf16[2,5,128,128]{3,2,1,0:T(8,128)(2,1)S(1)}, u32[]{:S(2)}, u32[]{:S(2)}) collective-permute-start(bf16[2,5,128,128]{3,2,1,0:T(8,128)(2,1)S(1)} %pad_maximum_fusion.3), channel_id=1, source_target_pairs={{0,16},{16,32},{32,48},{48,64},{64,80},{80,96},{96,112},{1,17},{17... | collective-permute-start | bytes 983048 | tf_op jit(solution)/shard_map/ppermute | solution.py:29
  55.0 0.7 copy-start.3
  61.9 0.7 copy-start.5
  62.3 0.7 copy-start.1
  78.1 5.9 %collective-permute-start.7 = (f32[2,2,2,2,2,13824]{5,4,3,2,1,0:T(2,128)}, f32[2,2,2,2,2,13824]{5,4,3,2,1,0:T(2,128)}, u32[]{:S(2)}, u32[]{:S(2)}) collective-permute-start(f32[2,2,2,2,2,13824]{5,4,3,2,1,0:T(2,128)} %dynamic-slice_bitcast_fusion), channel_id=1, source_target_pairs={{0,128},{128,0},{256,384},{384,256},{1,129},{129,1},{257,385},{385... | collective-permute-start | bytes 5308424 | tf_op jit(solution)/shard_map/ppermute | solution.py:175
  88.5 23.6 %collective-permute-start.8 = (f32[2,2,2,2,13824]{4,3,2,1,0:T(2,128)S(1)}, f32[2,2,2,2,13824]{4,3,2,1,0:T(2,128)S(1)}, u32[]{:S(2)}, u32[]{:S(2)}) collective-permute-start(f32[2,2,2,2,13824]{4,3,2,1,0:T(2,128)S(1)} %bitcast.224), channel_id=1, source_target_pairs={{0,1},{1,0},{2,3},{3,2},{4,5},{5,4},{6,7},{7,6},{8,9},{9,8},{10,11... | collective-permute-start | bytes 2654216 | tf_op jit(solution)/shard_map/ppermute | solution.py:175
  112.7 13.3 %collective-permute-start.9 = (f32[2,2,2,13824]{3,2,1,0:T(2,128)S(1)}, f32[2,2,2,13824]{3,2,1,0:T(2,128)S(1)}, u32[]{:S(2)}, u32[]{:S(2)}) collective-permute-start(f32[2,2,2,13824]{3,2,1,0:T(2,128)S(1)} %dynamic-slice_bitcast_fusion.1), channel_id=1, source_target_pairs={{0,4},{1,5},{2,6},{3,7},{4,0},{5,1},{6,2},{7,3},{8,12},{9,13},{10,... | collective-permute-start | bytes 1327112 | tf_op jit(solution)/shard_map/ppermute | solution.py:175
  115.2 44.2 %copy-start.8 = (bf16[3,3,3,128,128]{4,3,2,1,0:T(8,128)(2,1)S(1)}, bf16[3,3,3,128,128]{4,3,2,1,0:T(8,128)(2,1)}, u32[]{:S(2)}) copy-start(bf16[3,3,3,128,128]{4,3,2,1,0:T(8,128)(2,1)} %param.8) | copy-start | bytes 2654212
  126.6 47.5 %copy-start.2 = (bf16[1,2,64,1152]{3,2,1,0:T(8,128)(2,1)S(1)}, bf16[1,2,64,1152]{3,2,1,0:T(8,128)(2,1)}, u32[]{:S(2)}) copy-start(bf16[1,2,64,1152]{3,2,1,0:T(8,128)(2,1)} %copy-done.1) | copy-start | bytes 884740
  126.8 9.3 %collective-permute-start.10 = (f32[2,2,13824]{2,1,0:T(2,128)S(1)}, f32[2,2,13824]{2,1,0:T(2,128)S(1)}, u32[]{:S(2)}, u32[]{:S(2)}) collective-permute-start(f32[2,2,13824]{2,1,0:T(2,128)S(1)} %bitcast.237), channel_id=1, source_target_pairs={{0,2},{1,3},{2,0},{3,1},{4,6},{5,7},{6,4},{7,5},{8,10},{9,11},{10,... | collective-permute-start | bytes 663560 | tf_op jit(solution)/shard_map/ppermute | solution.py:175
  136.3 55.7 %copy-start.6 = (bf16[1,2,64,1152]{3,2,1,0:T(8,128)(2,1)S(1)}, bf16[1,2,64,1152]{3,2,1,0:T(8,128)(2,1)}, u32[]{:S(2)}) copy-start(bf16[1,2,64,1152]{3,2,1,0:T(8,128)(2,1)} %copy-done.5) | copy-start | bytes 884740
  136.5 8.1 %collective-permute-start.11 = (f32[2,13824]{1,0:T(2,128)S(1)}, f32[2,13824]{1,0:T(2,128)S(1)}, u32[]{:S(2)}, u32[]{:S(2)}) collective-permute-start(f32[2,13824]{1,0:T(2,128)S(1)} %bitcast.240), channel_id=1, source_target_pairs={{0,8},{1,9},{2,10},{3,11},{4,12},{5,13},{6,14},{7,15},{8,0},{9,1},... | collective-permute-start | bytes 331784 | tf_op jit(solution)/shard_map/ppermute | solution.py:175
  144.8 52.5 %copy-start.4 = (bf16[1,2,64,1152]{3,2,1,0:T(8,128)(2,1)S(1)}, bf16[1,2,64,1152]{3,2,1,0:T(8,128)(2,1)}, u32[]{:S(2)}) copy-start(bf16[1,2,64,1152]{3,2,1,0:T(8,128)(2,1)} %copy-done.3) | copy-start | bytes 884740
  144.8 7.2 %collective-permute-start.12 = (f32[2,13824]{1,0:T(2,128)S(1)}, f32[2,13824]{1,0:T(2,128)S(1)}, u32[]{:S(2)}, u32[]{:S(2)}) collective-permute-start(f32[2,13824]{1,0:T(2,128)S(1)} %bitcast_add_fusion.4), channel_id=1, source_target_pairs={{0,16},{16,0},{32,48},{48,32},{64,80},{80,64},{96,112},{112,96},{1... | collective-permute-start | bytes 331784 | tf_op jit(solution)/shard_map/ppermute | solution.py:175
  152.1 10.0 %collective-permute-start.13 = (f32[2,13824]{1,0:T(2,128)S(1)}, f32[2,13824]{1,0:T(2,128)S(1)}, u32[]{:S(2)}, u32[]{:S(2)}) collective-permute-start(f32[2,13824]{1,0:T(2,128)S(1)} %add.195), channel_id=1, source_target_pairs={{0,32},{16,48},{32,0},{48,16},{64,96},{80,112},{96,64},{112,80},{1... | collective-permute-start | bytes 331784 | tf_op jit(solution)/shard_map/ppermute | solution.py:175
  162.1 16.0 %collective-permute-start.14 = (f32[2,13824]{1,0:T(2,128)S(1)}, f32[2,13824]{1,0:T(2,128)S(1)}, u32[]{:S(2)}, u32[]{:S(2)}) collective-permute-start(f32[2,13824]{1,0:T(2,128)S(1)} %add.196), channel_id=1, source_target_pairs={{0,64},{16,80},{32,96},{48,112},{64,0},{80,16},{96,32},{112,48},{1... | collective-permute-start | bytes 331784 | tf_op jit(solution)/shard_map/ppermute | solution.py:175
  178.5 15.7 %collective-permute-start.15 = (f32[13824]{0:T(1024)S(1)}, f32[13824]{0:T(1024)S(1)}, u32[]{:S(2)}, u32[]{:S(2)}) collective-permute-start(f32[13824]{0:T(1024)S(1)} %get-tuple-element.3), channel_id=1, source_target_pairs={{0,256},{128,384},{256,0},{384,128},{1,257},{129,385},{257,1},{385... | collective-permute-start | bytes 165896 | tf_op jit(solution)/shard_map/ppermute | solution.py:175
  194.2 7.3 %collective-permute-start.16 = (bf16[13824]{0:T(1024)(128)(2,1)S(1)}, bf16[13824]{0:T(1024)(128)(2,1)S(1)}, u32[]{:S(2)}, u32[]{:S(2)}) collective-permute-start(bf16[13824]{0:T(1024)(128)(2,1)S(1)} %add_convert_fusion), channel_id=1, source_target_pairs={{0,8},{1,9},{2,10},{3,11},{4,12},{5,13},{6,14},{7,15},{8,0},{9,1},... | collective-permute-start | bytes 82952 | tf_op jit(solution)/shard_map/ppermute | solution.py:175
  201.8 7.6 %collective-permute-start.17 = (bf16[2,13824]{1,0:T(2,128)(2,1)S(1)}, bf16[2,13824]{1,0:T(2,128)(2,1)S(1)}, u32[]{:S(2)}, u32[]{:S(2)}) collective-permute-start(bf16[2,13824]{1,0:T(2,128)(2,1)S(1)} %broadcast_select_fusion.5), channel_id=1, source_target_pairs={{0,2},{1,3},{2,0},{3,1},{4,6},{5,7},{6,4},{7,5},{8,10},{9,11},{10,... | collective-permute-start | bytes 165896 | tf_op jit(solution)/shard_map/ppermute | solution.py:175
  209.5 6.6 %collective-permute-start.18 = (bf16[2,2,13824]{2,0,1:T(2,128)(2,1)S(1)}, bf16[2,2,13824]{2,0,1:T(2,128)(2,1)S(1)}, u32[]{:S(2)}, u32[]{:S(2)}) collective-permute-start(bf16[2,2,13824]{2,0,1:T(2,128)(2,1)S(1)} %broadcast_select_fusion.3), channel_id=1, source_target_pairs={{0,4},{1,5},{2,6},{3,7},{4,0},{5,1},{6,2},{7,3},{8,12},{9,13},{10,... | collective-permute-start | bytes 331784 | tf_op jit(solution)/shard_map/ppermute | solution.py:175
  216.5 7.9 %collective-permute-start.19 = (bf16[2,2,2,13824]{3,0,2,1:T(2,128)(2,1)S(1)}, bf16[2,2,2,13824]{3,0,2,1:T(2,128)(2,1)S(1)}, u32[]{:S(2)}, u32[]{:S(2)}) collective-permute-start(bf16[2,2,2,13824]{3,0,2,1:T(2,128)(2,1)S(1)} %broadcast_select_fusion.1), channel_id=1, source_target_pairs={{0,1},{1,0},{2,3},{3,2},{4,5},{5,4},{6,7},{7,6},{8,9},{9,8},{10,11... | collective-permute-start | bytes 663560 | tf_op jit(solution)/shard_map/ppermute | solution.py:175
